TPU v7x, 512 devices: a whole 4x8x8 slice. The times are simulated.
512 devices in a mesh: diag: 64 (over z_lo, y, x), off: 8 (over z_hi, core).
Axes of the slice: x: 4, y: 8, z: 8 (z_hi: 4, z_lo: 2; z = z_hi * 2 + z_lo), core: 2. Of those that a mesh axis runs over, the one named last changes fastest.
Arguments:
- trunk: bfloat16 [64, 1, 64, 128], P('diag'), may hold values from -6 to 6
- w_first: bfloat16 [48, 128, 3, 3], replicated, may hold values from -0.1875 to 0.1875
- b_first: float32 [48], replicated, may hold values from -3 to 3
- w_second: bfloat16 [48, 48, 3, 3], replicated, may hold values from -0.3125 to 0.3125
- b_second: float32 [48], replicated, may hold values from -3 to 3
Outputs:
- contact_tiles: bfloat16 [64, 8, 1, 48, 128, 128], P('diag', 'off')
All inputs are finite; a program needn't handle non-finite values.
Results may differ from a plain program's by a relative error of at most 0.0043.
Values may be sent and summed in bfloat16 or wider, within the bound.
No kernel may reach another device: no remote copies, remote signals or barrier semaphores. Data moves between devices by JAX's collectives and lax.ppermute only.
A program may use at most 128 MiB of HBM per device.

v0:
```python
import jax
import jax.numpy as jnp
from jax import lax
from jax.sharding import PartitionSpec as P


def from_behind(shard, axis, by):
    length = lax.axis_size(axis)
    pairs = [(i, i + by) for i in range(length) if 0 <= i + by < length]
    return lax.ppermute(shard, axis, pairs)


def band_mask(row_tile, col_tile, start, extent, width, nbins, offsets_total):
    offsets = start + jnp.arange(extent, dtype=jnp.int32)
    row_bins = row_tile * width + offsets
    col_bins = col_tile * width + offsets
    row_ok = (row_bins >= 0) & (row_bins < nbins)
    col_ok = (col_bins >= 0) & (col_bins < nbins)
    gap = jnp.floor_divide(col_bins, width)[None, :] - jnp.floor_divide(row_bins, width)[:, None]
    return row_ok[:, None] & col_ok[None, :] & (gap >= 0) & (gap < offsets_total)


def neighbour(piece, by, keep):
    moved = from_behind(piece, ("diag", "off"), by)
    return jnp.where(keep, moved, jnp.zeros_like(moved))


def local(trunk, w_first, b_first, w_second, b_second):
    samples = trunk.shape[1]
    channels = trunk.shape[2]
    width = trunk.shape[3]
    hidden_width = w_first.shape[0]
    offsets_total = lax.axis_size("off")
    nbins = lax.axis_size("diag") * width
    row_tile = lax.axis_index("diag")
    offset = lax.axis_index("off")
    col_tile = row_tile + offset
    ahead = trunk
    length = 1
    while length < offsets_total + 1:
        moved = from_behind(ahead, "diag", -length)
        ahead = jnp.concatenate([ahead, moved], axis=0)
        length = length * 2
    below = from_behind(trunk, "diag", 1)
    window = jnp.concatenate([below, ahead[: offsets_total + 1]], axis=0)
    line = jnp.transpose(window, (1, 2, 0, 3)).reshape(
        samples, channels, (offsets_total + 2) * width
    )
    reach = 2
    extent = width + 2 * reach
    inner_size = extent - 4
    rows = line[:, :, width - reach : width - reach + extent]
    cols = lax.dynamic_slice_in_dim(line, (1 + offset) * width - reach, extent, 2)
    outer_mask = band_mask(row_tile, col_tile, -reach, extent, width, nbins, offsets_total)
    pre = jnp.zeros((samples, hidden_width, inner_size, inner_size), jnp.float32)
    features = jnp.concatenate(
        [
            jnp.broadcast_to(rows[:, :, :, None], (samples, channels, extent, extent)),
            jnp.broadcast_to(cols[:, :, None, :], (samples, channels, extent, extent)),
        ],
        axis=1,
    )
    features = jnp.where(outer_mask[None, None], features, jnp.zeros_like(features))
    for tap_row in range(3):
        for tap_col in range(3):
            window_cells = features[
                :, :, 2 * tap_row : 2 * tap_row + inner_size, 2 * tap_col : 2 * tap_col + inner_size
            ]
            pre = pre + jnp.einsum(
                "hc,bcij->bhij",
                w_first[:, :, tap_row, tap_col],
                window_cells,
                preferred_element_type=jnp.float32,
            )
    inner_mask = band_mask(row_tile, col_tile, 2 - reach, inner_size, width, nbins, offsets_total)
    hidden = jnp.where(
        inner_mask[None, None], jnp.maximum(pre + b_first[None, :, None, None], 0.0), 0.0
    )
    hidden = hidden.astype(jnp.bfloat16)
    low_rows = hidden[:, :, width - 4 :, :]
    high_rows = hidden[:, :, :4, :]
    top_left = neighbour(low_rows[:, :, :, width - 4 :], offsets_total, True)
    top_mid = neighbour(low_rows, offsets_total - 1, offset < offsets_total - 1)
    bottom_mid = neighbour(high_rows, -(offsets_total - 1), offset > 0)
    bottom_right = neighbour(high_rows[:, :, :, :4], -offsets_total, True)
    top_right = neighbour(low_rows[:, :, :, :4], offsets_total - 2, offset < offsets_total - 2)
    bottom_left = neighbour(high_rows[:, :, :, width - 4 :], -(offsets_total - 2), offset > 1)
    left = neighbour(hidden[:, :, :, width - 4 :], 1, offset > 0)
    right = neighbour(hidden[:, :, :, :4], -1, offset < offsets_total - 1)
    upper = jnp.concatenate([top_left, top_mid, top_right], axis=3)
    middle = jnp.concatenate([left, hidden, right], axis=3)
    lower = jnp.concatenate([bottom_left, bottom_mid, bottom_right], axis=3)
    hidden = jnp.concatenate([upper, middle, lower], axis=2)
    result = jnp.zeros((samples, hidden_width, width, width), jnp.float32)
    for tap_row in range(3):
        for tap_col in range(3):
            window_cells = hidden[
                :, :, 4 * tap_row : 4 * tap_row + width, 4 * tap_col : 4 * tap_col + width
            ]
            result = result + jnp.einsum(
                "hk,bkij->bhij",
                w_second[:, :, tap_row, tap_col],
                window_cells,
                preferred_element_type=jnp.float32,
            )
    result = (result + b_second[None, :, None, None]).astype(jnp.bfloat16)
    return result[None, None]


def solution(mesh):
    placed = (P("diag", None, None, None), P(), P(), P(), P())
    return jax.shard_map(
        local,
        mesh=mesh,
        in_specs=placed,
        out_specs=P("diag", "off", None, None, None, None),
        check_vma=False,
    )
```

profile of v0, /device:TPU:193, one launch (start us, length us, event | category | flops | bytes accessed | tf_op | source)
XLA Modules:
  0.0 167.2 jit_solution(9570024623117360991)
XLA Ops:
  0.0 6.4 %collective-permute-start.1 = (bf16[1,1,64,128]{3,2,1,0:T(8,128)(2,1)}, bf16[1,1,64,128]{3,2,1,0:T(8,128)(2,1)S(1)}, u32[]{:S(2)}, u32[]{:S(2)}) collective-permute-start(bf16[1,1,64,128]{3,2,1,0:T(8,128)(2,1)} %param.5), channel_id=1, source_target_pairs={{8,0},{16,8},{24,16},{32,24},{40,32},{48,40},{56,48},{64,56},{72,6... | collective-permute-start | bytes 49160 | tf_op jit(solution)/shard_map/ppermute | solution.py:10
  9.4 3.6 %collective-permute-start.2 = (bf16[2,1,64,128]{3,2,1,0:T(8,128)(2,1)S(1)}, bf16[2,1,64,128]{3,2,1,0:T(8,128)(2,1)S(1)}, u32[]{:S(2)}, u32[]{:S(2)}) collective-permute-start(bf16[2,1,64,128]{3,2,1,0:T(8,128)(2,1)S(1)} %pad_maximum_fusion.4), channel_id=1, source_target_pairs={{16,0},{24,8},{32,16},{40,24},{48,32},{56,40},{64,48},{72,56},{80,... | collective-permute-start | bytes 98312 | tf_op jit(solution)/shard_map/ppermute | solution.py:10
  16.4 2.8 %collective-permute-start.3 = (bf16[4,1,64,128]{3,2,1,0:T(8,128)(2,1)S(1)}, bf16[4,1,64,128]{3,2,1,0:T(8,128)(2,1)S(1)}, u32[]{:S(2)}, u32[]{:S(2)}) collective-permute-start(bf16[4,1,64,128]{3,2,1,0:T(8,128)(2,1)S(1)} %pad_maximum_fusion.3), channel_id=1, source_target_pairs={{32,0},{40,8},{48,16},{56,24},{64,32},{72,40},{80,48},{88,56},{96,... | collective-permute-start | bytes 196616 | tf_op jit(solution)/shard_map/ppermute | solution.py:10
  22.1 3.6 %collective-permute-start.4 = (bf16[8,1,64,128]{3,2,1,0:T(8,128)(2,1)S(1)}, bf16[8,1,64,128]{3,2,1,0:T(8,128)(2,1)S(1)}, u32[]{:S(2)}, u32[]{:S(2)}) collective-permute-start(bf16[8,1,64,128]{3,2,1,0:T(8,128)(2,1)S(1)} %pad_maximum_fusion.2), channel_id=1, source_target_pairs={{64,0},{72,8},{80,16},{88,24},{96,32},{104,40},{112,48},{120,56},{... | collective-permute-start | bytes 393224 | tf_op jit(solution)/shard_map/ppermute | solution.py:10
  25.8 4.3 %collective-permute-done.4 = bf16[8,1,64,128]{3,2,1,0:T(8,128)(2,1)S(1)} collective-permute-done((bf16[8,1,64,128]{3,2,1,0:T(8,128)(2,1)S(1)}, bf16[8,1,64,128]{3,2,1,0:T(8,128)(2,1)S(1)}, u32[]{:S(2)}, u32[]{:S(2)}) %collective-permute-start.4) | collective-permute-done | bytes 131104 | tf_op jit(solution)/shard_map/ppermute | solution.py:10
  32.5 3.0 %maximum_select_fusion = bf16[1,128,132,132]{3,1,2,0:T(8,128)(2,1)S(1)} fusion(bf16[1,64,132,132]{3,1,2,0:T(8,128)(2,1)S(1)} %broadcast_in_dim.35, bf16[1,64,132,132]{3,1,2,0:T(8,128)(2,1)S(1)} %broadcast_in_dim.29, pred[132,132]{1,0:T(8,128)(4,1)S(1)} %fusion.30), kind=kLoop, calls=%fused_computation | loop fusion | flops 11151360 | bytes 8938512 | tf_op jit(solution)/shard_map/jit(_where)/select_n | solution.py:63
  37.0 3.2 %fusion.1 = f32[128,128,48]{1,2,0:T(8,128)} fusion(bf16[1,128,132,132]{3,1,2,0:T(8,128)(2,1)S(1)} %maximum_select_fusion, bf16[48,128,3,3]{1,0,3,2:T(8,128)(2,1)S(1)} %copy-done.3), kind=kOutput, calls=%fused_computation.4 | convolution fusion | flops 201326592 | bytes 7352320 | tf_op jit(solution)/shard_map/hc,bcij->bhij/dot_general | solution.py:69
  40.2 2.4 %fusion.2 = f32[128,128,48]{1,2,0:T(8,128)} fusion(bf16[1,128,132,132]{3,1,2,0:T(8,128)(2,1)S(1)} %maximum_select_fusion, bf16[48,128,3,3]{1,0,3,2:T(8,128)(2,1)S(1)} %copy-done.3), kind=kOutput, calls=%fused_computation.6 | convolution fusion | flops 201326592 | bytes 7352320 | tf_op jit(solution)/shard_map/hc,bcij->bhij/dot_general | solution.py:69
  42.6 3.3 %fusion.3 = f32[128,128,48]{1,2,0:T(8,128)} fusion(bf16[1,128,132,132]{3,1,2,0:T(8,128)(2,1)S(1)} %maximum_select_fusion, bf16[48,128,3,3]{1,0,3,2:T(8,128)(2,1)S(1)} %copy-done.3), kind=kOutput, calls=%fused_computation.8 | convolution fusion | flops 201326592 | bytes 7352320 | tf_op jit(solution)/shard_map/hc,bcij->bhij/dot_general | solution.py:69
  45.8 3.2 %fusion.4 = f32[128,128,48]{1,2,0:T(8,128)} fusion(bf16[1,128,132,132]{3,1,2,0:T(8,128)(2,1)S(1)} %maximum_select_fusion, bf16[48,128,3,3]{1,0,3,2:T(8,128)(2,1)S(1)} %copy-done.3), kind=kOutput, calls=%fused_computation.10 | convolution fusion | flops 201326592 | bytes 7352320 | tf_op jit(solution)/shard_map/hc,bcij->bhij/dot_general | solution.py:69
  51.4 3.2 %fusion.6 = f32[128,128,48]{1,2,0:T(8,128)} fusion(bf16[1,128,132,132]{3,1,2,0:T(8,128)(2,1)S(1)} %maximum_select_fusion, bf16[48,128,3,3]{1,0,3,2:T(8,128)(2,1)S(1)} %copy-done.3), kind=kOutput, calls=%fused_computation.14 | convolution fusion | flops 201326592 | bytes 7352320 | tf_op jit(solution)/shard_map/hc,bcij->bhij/dot_general | solution.py:69
  54.6 3.3 %fusion.7 = f32[128,128,48]{1,2,0:T(8,128)} fusion(bf16[1,128,132,132]{3,1,2,0:T(8,128)(2,1)S(1)} %maximum_select_fusion, bf16[48,128,3,3]{1,0,3,2:T(8,128)(2,1)S(1)} %copy-done.3), kind=kOutput, calls=%fused_computation.16 | convolution fusion | flops 201326592 | bytes 7352320 | tf_op jit(solution)/shard_map/hc,bcij->bhij/dot_general | solution.py:69
  57.9 8.7 %fusion.12 = bf16[1,128,128,48]{2,3,1,0:T(8,128)(2,1)S(1)} fusion(f32[128,128,48]{1,2,0:T(8,128)S(1)} %fusion, f32[128,128,48]{1,2,0:T(8,128)} %fusion.1, f32[128,128,48]{1,2,0:T(8,128)} %fusion.2, f32[128,128,48]{1,2,0:T(8,128)} %fusion.3, f32[128,128,48]{1,2,0:T(8,128)} %fusion.4, f32[128,128,48]{1,2,0:T(8,128)} %fusion.5, f32[128,128,48]{1,2,0:T(8,128)} %fusion.6, ...), kind=kOutput, calls=%fused_computation.26 | convolution fusion | flops 210763776 | bytes 30962176 | tf_op jit(solution)/shard_map/hc,bcij->bhij/dot_general | solution.py:69
  69.0 2.8 %copy.13 = bf16[1,48,128,4]{2,1,3,0:T(8,128)(2,1)} copy(bf16[1,48,128,4]{3,1,2,0:T(8,128)(2,1)} %get-tuple-element.13) | data formatting | bytes 98304 | tf_op jit(solution)/shard_map/slice | solution.py:88
  71.8 10.5 %collective-permute-start.8 = (bf16[1,48,128,4]{2,1,3,0:T(8,128)(2,1)}, bf16[1,48,128,4]{2,1,3,0:T(8,128)(2,1)}, u32[]{:S(2)}, u32[]{:S(2)}) collective-permute-start(bf16[1,48,128,4]{2,1,3,0:T(8,128)(2,1)} %copy.13), channel_id=1, source_target_pairs={{0,1},{1,2},{2,3},{3,4},{4,5},{5,6},{6,7},{7,8},{8,9},{9,10},{10,1... | collective-permute-start | bytes 147464 | tf_op jit(solution)/shard_map/ppermute | solution.py:10
  85.3 15.4 %collective-permute-start.10 = (bf16[1,48,4,4]{3,1,2,0:T(8,128)(2,1)S(1)}, bf16[1,48,4,4]{3,1,2,0:T(8,128)(2,1)S(1)}, u32[]{:S(2)}, u32[]{:S(2)}) collective-permute-start(bf16[1,48,4,4]{3,1,2,0:T(8,128)(2,1)S(1)} %get-tuple-element.8), channel_id=1, source_target_pairs={{6,0},{7,1},{8,2},{9,3},{10,4},{11,5},{12,6},{13,7},{14,8},{15,9},... | collective-permute-start | bytes 4616 | tf_op jit(solution)/shard_map/ppermute | solution.py:10
  102.6 6.7 %collective-permute-start.12 = (bf16[1,48,4,4]{3,1,2,0:T(8,128)(2,1)}, bf16[1,48,4,4]{3,1,2,0:T(8,128)(2,1)S(1)}, u32[]{:S(2)}, u32[]{:S(2)}) collective-permute-start(bf16[1,48,4,4]{3,1,2,0:T(8,128)(2,1)} %get-tuple-element.9), channel_id=1, source_target_pairs={{8,0},{9,1},{10,2},{11,3},{12,4},{13,5},{14,6},{15,7},{16,8},{17,9... | collective-permute-start | bytes 4616 | tf_op jit(solution)/shard_map/ppermute | solution.py:10
  114.0 12.6 %collective-permute-start.11 = (bf16[1,48,4,128]{3,1,2,0:T(8,128)(2,1)}, bf16[1,48,4,128]{3,1,2,0:T(8,128)(2,1)}, u32[]{:S(2)}, u32[]{:S(2)}) collective-permute-start(bf16[1,48,4,128]{3,1,2,0:T(8,128)(2,1)} %get-tuple-element.12), channel_id=1, source_target_pairs={{7,0},{8,1},{9,2},{10,3},{11,4},{12,5},{13,6},{14,7},{15,8},{16,9}... | collective-permute-start | bytes 147464 | tf_op jit(solution)/shard_map/ppermute | solution.py:10
  128.6 2.5 %copy.14 = bf16[1,48,128,4]{3,1,2,0:T(8,128)(2,1)} copy(bf16[1,48,128,4]{2,1,3,0:T(8,128)(2,1)} %collective-permute-done.8) | data formatting | bytes 98304 | tf_op jit(solution)/shard_map/ppermute | solution.py:10
  132.6 2.6 %fusion.20 = f32[128,128,48]{1,2,0:T(8,128)} fusion(bf16[1,48,128,128]{3,1,2,0:T(8,128)(2,1)S(1)} %bitcast.181, bf16[1,48,128,4]{3,1,2,0:T(8,128)(2,1)S(1)} %broadcast_select_fusion.1, bf16[48,48,3,3]{1,0,3,2:T(8,128)(2,1)S(1)} %copy-done.2), kind=kOutput, calls=%fused_computation.38 | convolution fusion | flops 78643200 | bytes 6303744 | tf_op jit(solution)/shard_map/hk,bkij->bhij/dot_general | solution.py:100
  141.2 9.7 %maximum_maximum_fusion = (bf16[1,48,132,136]{3,1,2,0:T(8,128)(2,1)S(1)}, bf16[1,48,132,136]{3,1,2,0:T(8,128)(2,1)S(1)}) fusion(bf16[1,48,128,4]{3,1,2,0:T(8,128)(2,1)S(1)} %broadcast_select_fusion, bf16[1,48,128,128]{3,1,2,0:T(8,128)(2,1)S(1)} %bitcast.183, bf16[1,48,128,4]{3,1,2,0:T(8,128)(2,1)S(1)} %broadcast_select_fusion.1, ...), kind=kLoop, calls=%fused_computation.19 | loop fusion | flops 20680704 | bytes 5222400 | tf_op jit(solution)/shard_map/concatenate | solution.py:93
  152.2 2.4 %fusion.23 = f32[128,128,48]{1,2,0:T(8,128)} fusion(bf16[1,48,132,136]{3,1,2,0:T(8,128)(2,1)S(1)} %get-tuple-element.5, bf16[48,48,3,3]{1,0,3,2:T(8,128)(2,1)S(1)} %copy-done.2), kind=kOutput, calls=%fused_computation.41 | convolution fusion | flops 75497472 | bytes 4730880 | tf_op jit(solution)/shard_map/hk,bkij->bhij/dot_general | solution.py:100
  154.6 2.4 %fusion.24 = f32[128,128,48]{1,2,0:T(8,128)} fusion(bf16[1,48,132,136]{3,1,2,0:T(8,128)(2,1)S(1)} %get-tuple-element.5, bf16[48,48,3,3]{1,0,3,2:T(8,128)(2,1)S(1)} %copy-done.2), kind=kOutput, calls=%fused_computation.43 | convolution fusion | flops 75497472 | bytes 4730880 | tf_op jit(solution)/shard_map/hk,bkij->bhij/dot_general | solution.py:100
  159.7 6.0 %fusion.28 = bf16[1,1,1,48,128,128]{5,3,4,2,1,0:T(8,128)(2,1)S(1)} fusion(f32[48]{0:T(128)S(1)} %copy-done.5, bf16[1,48,132,136]{3,1,2,0:T(8,128)(2,1)S(1)} %get-tuple-element.6, f32[128,128,48]{1,2,0:T(8,128)S(1)} %fusion.13, f32[128,128,48]{1,2,0:T(8,128)S(1)} %fusion.14, f32[128,128,48]{1,2,0:T(8,128)S(1)} %fusion.16, f32[128,128,48]{1,2,0:T(8,128)S(1)} %copy-done, ...), kind=kOutput, calls=%fused_computation.50 | convolution fusion | flops 83361792 | bytes 28324352 | tf_op jit(solution)/shard_map/hk,bkij->bhij/dot_general | solution.py:100
  (68 shorter events, 42.6 us)
Async XLA Ops:
  0.0 8.6 %collective-permute-start.1 = (bf16[1,1,64,128]{3,2,1,0:T(8,128)(2,1)}, bf16[1,1,64,128]{3,2,1,0:T(8,128)(2,1)S(1)}, u32[]{:S(2)}, u32[]{:S(2)}) collective-permute-start(bf16[1,1,64,128]{3,2,1,0:T(8,128)(2,1)} %param.5), channel_id=1, source_target_pairs={{8,0},{16,8},{24,16},{32,24},{40,32},{48,40},{56,48},{64,56},{72,6... | collective-permute-start | bytes 49160 | tf_op jit(solution)/shard_map/ppermute | solution.py:10
  6.4 23.7 %collective-permute-start = (bf16[1,1,64,128]{3,2,1,0:T(8,128)(2,1)}, bf16[1,1,64,128]{3,2,1,0:T(8,128)(2,1)S(1)}, u32[]{:S(2)}, u32[]{:S(2)}) collective-permute-start(bf16[1,1,64,128]{3,2,1,0:T(8,128)(2,1)} %param.5), channel_id=1, source_target_pairs={{0,8},{8,16},{16,24},{24,32},{32,40},{40,48},{48,56},{56,64},{64,7... | collective-permute-start | bytes 49160 | tf_op jit(solution)/shard_map/ppermute | solution.py:10
  9.4 6.3 %collective-permute-start.2 = (bf16[2,1,64,128]{3,2,1,0:T(8,128)(2,1)S(1)}, bf16[2,1,64,128]{3,2,1,0:T(8,128)(2,1)S(1)}, u32[]{:S(2)}, u32[]{:S(2)}) collective-permute-start(bf16[2,1,64,128]{3,2,1,0:T(8,128)(2,1)S(1)} %pad_maximum_fusion.4), channel_id=1, source_target_pairs={{16,0},{24,8},{32,16},{40,24},{48,32},{56,40},{64,48},{72,56},{80,... | collective-permute-start | bytes 98312 | tf_op jit(solution)/shard_map/ppermute | solution.py:10
  16.4 5.0 %collective-permute-start.3 = (bf16[4,1,64,128]{3,2,1,0:T(8,128)(2,1)S(1)}, bf16[4,1,64,128]{3,2,1,0:T(8,128)(2,1)S(1)}, u32[]{:S(2)}, u32[]{:S(2)}) collective-permute-start(bf16[4,1,64,128]{3,2,1,0:T(8,128)(2,1)S(1)} %pad_maximum_fusion.3), channel_id=1, source_target_pairs={{32,0},{40,8},{48,16},{56,24},{64,32},{72,40},{80,48},{88,56},{96,... | collective-permute-start | bytes 196616 | tf_op jit(solution)/shard_map/ppermute | solution.py:10
  22.1 7.9 %collective-permute-start.4 = (bf16[8,1,64,128]{3,2,1,0:T(8,128)(2,1)S(1)}, bf16[8,1,64,128]{3,2,1,0:T(8,128)(2,1)S(1)}, u32[]{:S(2)}, u32[]{:S(2)}) collective-permute-start(bf16[8,1,64,128]{3,2,1,0:T(8,128)(2,1)S(1)} %pad_maximum_fusion.2), channel_id=1, source_target_pairs={{64,0},{72,8},{80,16},{88,24},{96,32},{104,40},{112,48},{120,56},{... | collective-permute-start | bytes 393224 | tf_op jit(solution)/shard_map/ppermute | solution.py:10
  32.5 3.0 %copy-start.3 = (bf16[48,128,3,3]{1,0,3,2:T(8,128)(2,1)S(1)}, bf16[48,128,3,3]{1,0,3,2:T(8,128)(2,1)}, u32[]{:S(2)}) copy-start(bf16[48,128,3,3]{1,0,3,2:T(8,128)(2,1)} %param.6) | copy-start | bytes 331780
  54.6 3.3 %copy-start.4 = (f32[48]{0:T(128)S(1)}, f32[48]{0:T(128)}, u32[]{:S(2)}) copy-start(f32[48]{0:T(128)} %param.7) | copy-start | bytes 580
  68.3 40.9 %copy-start.2 = (bf16[48,48,3,3]{1,0,3,2:T(8,128)(2,1)S(1)}, bf16[48,48,3,3]{1,0,3,2:T(8,128)(2,1)}, u32[]{:S(2)}) copy-start(bf16[48,48,3,3]{1,0,3,2:T(8,128)(2,1)} %param.8) | copy-start | bytes 124420
  71.8 54.8 %collective-permute-start.8 = (bf16[1,48,128,4]{2,1,3,0:T(8,128)(2,1)}, bf16[1,48,128,4]{2,1,3,0:T(8,128)(2,1)}, u32[]{:S(2)}, u32[]{:S(2)}) collective-permute-start(bf16[1,48,128,4]{2,1,3,0:T(8,128)(2,1)} %copy.13), channel_id=1, source_target_pairs={{0,1},{1,2},{2,3},{3,4},{4,5},{5,6},{6,7},{7,8},{8,9},{9,10},{10,1... | collective-permute-start | bytes 147464 | tf_op jit(solution)/shard_map/ppermute | solution.py:10
  83.4 51.8 %collective-permute-start.9 = (bf16[1,48,128,4]{2,1,3,0:T(8,128)(2,1)S(1)}, bf16[1,48,128,4]{2,1,3,0:T(8,128)(2,1)S(1)}, u32[]{:S(2)}, u32[]{:S(2)}) collective-permute-start(bf16[1,48,128,4]{2,1,3,0:T(8,128)(2,1)S(1)} %copy.15), channel_id=1, source_target_pairs={{1,0},{2,1},{3,2},{4,3},{5,4},{6,5},{7,6},{8,7},{9,8},{10,9},{11,1... | collective-permute-start | bytes 147464 | tf_op jit(solution)/shard_map/ppermute | solution.py:10
  85.3 26.8 %collective-permute-start.10 = (bf16[1,48,4,4]{3,1,2,0:T(8,128)(2,1)S(1)}, bf16[1,48,4,4]{3,1,2,0:T(8,128)(2,1)S(1)}, u32[]{:S(2)}, u32[]{:S(2)}) collective-permute-start(bf16[1,48,4,4]{3,1,2,0:T(8,128)(2,1)S(1)} %get-tuple-element.8), channel_id=1, source_target_pairs={{6,0},{7,1},{8,2},{9,3},{10,4},{11,5},{12,6},{13,7},{14,8},{15,9},... | collective-permute-start | bytes 4616 | tf_op jit(solution)/shard_map/ppermute | solution.py:10
  100.7 13.4 %collective-permute-start.7 = (bf16[1,48,4,4]{3,1,2,0:T(8,128)(2,1)S(1)}, bf16[1,48,4,4]{3,1,2,0:T(8,128)(2,1)S(1)}, u32[]{:S(2)}, u32[]{:S(2)}) collective-permute-start(bf16[1,48,4,4]{3,1,2,0:T(8,128)(2,1)S(1)} %get-tuple-element.10), channel_id=1, source_target_pairs={{0,6},{1,7},{2,8},{3,9},{4,10},{5,11},{6,12},{7,13},{8,14},{9,15},... | collective-permute-start | bytes 4616 | tf_op jit(solution)/shard_map/ppermute | solution.py:10
  102.6 38.6 %collective-permute-start.12 = (bf16[1,48,4,4]{3,1,2,0:T(8,128)(2,1)}, bf16[1,48,4,4]{3,1,2,0:T(8,128)(2,1)S(1)}, u32[]{:S(2)}, u32[]{:S(2)}) collective-permute-start(bf16[1,48,4,4]{3,1,2,0:T(8,128)(2,1)} %get-tuple-element.9), channel_id=1, source_target_pairs={{8,0},{9,1},{10,2},{11,3},{12,4},{13,5},{14,6},{15,7},{16,8},{17,9... | collective-permute-start | bytes 4616 | tf_op jit(solution)/shard_map/ppermute | solution.py:10
  112.1 29.1 %collective-permute-start.5 = (bf16[1,48,4,4]{3,1,2,0:T(8,128)(2,1)}, bf16[1,48,4,4]{3,1,2,0:T(8,128)(2,1)S(1)}, u32[]{:S(2)}, u32[]{:S(2)}) collective-permute-start(bf16[1,48,4,4]{3,1,2,0:T(8,128)(2,1)} %get-tuple-element.7), channel_id=1, source_target_pairs={{0,8},{1,9},{2,10},{3,11},{4,12},{5,13},{6,14},{7,15},{8,16},{9,17... | collective-permute-start | bytes 4616 | tf_op jit(solution)/shard_map/ppermute | solution.py:10
  114.0 25.5 %collective-permute-start.11 = (bf16[1,48,4,128]{3,1,2,0:T(8,128)(2,1)}, bf16[1,48,4,128]{3,1,2,0:T(8,128)(2,1)}, u32[]{:S(2)}, u32[]{:S(2)}) collective-permute-start(bf16[1,48,4,128]{3,1,2,0:T(8,128)(2,1)} %get-tuple-element.12), channel_id=1, source_target_pairs={{7,0},{8,1},{9,2},{10,3},{11,4},{12,5},{13,6},{14,7},{15,8},{16,9}... | collective-permute-start | bytes 147464 | tf_op jit(solution)/shard_map/ppermute | solution.py:10
  126.7 13.7 %collective-permute-start.6 = (bf16[1,48,4,128]{3,1,2,0:T(8,128)(2,1)}, bf16[1,48,4,128]{3,1,2,0:T(8,128)(2,1)}, u32[]{:S(2)}, u32[]{:S(2)}) collective-permute-start(bf16[1,48,4,128]{3,1,2,0:T(8,128)(2,1)} %get-tuple-element.11), channel_id=1, source_target_pairs={{0,7},{1,8},{2,9},{3,10},{4,11},{5,12},{6,13},{7,14},{8,15},{9,16}... | collective-permute-start | bytes 147464 | tf_op jit(solution)/shard_map/ppermute | solution.py:10
  154.6 4.6 %copy-start.1 = (f32[128,128,48]{1,2,0:T(8,128)S(1)}, f32[128,128,48]{1,2,0:T(8,128)}, u32[]{:S(2)}) copy-start(f32[128,128,48]{1,2,0:T(8,128)} %fusion.20) | copy-start | bytes 9437188
  157.0 2.8 %copy-start = (f32[128,128,48]{1,2,0:T(8,128)S(1)}, f32[128,128,48]{1,2,0:T(8,128)}, u32[]{:S(2)}) copy-start(f32[128,128,48]{1,2,0:T(8,128)} %fusion.26) | copy-start | bytes 9437188
  157.0 2.8 %copy-start.5 = (f32[48]{0:T(128)S(1)}, f32[48]{0:T(128)}, u32[]{:S(2)}) copy-start(f32[48]{0:T(128)} %param.9) | copy-start | bytes 580
where the time goes:
time: 168 us; the launch traced here: 167 us
  starting transfers between devices  71.1 us (42%)
  matrix products  51.3 us (31%)
  other arithmetic  19.8 us (12%)
  local copies, waits for them, and re-layouts  16.3 us (10%)
  waiting for transfers between devices  8.39 us (5%)
    ppermute x13, starting transfers between devices, from_behind(): return lax.ppermute(shard, axis, pairs)  71.1 us
    dot_general x9, matrix products, local(): jnp.einsum('hc,bcij->bhij', w_first[:, :, tap_row, tap_col], window_cells...  31.2 us
    dot_general x9, matrix products, local(): jnp.einsum('hk,bkij->bhij', w_second[:, :, tap_row, tap_col], window_cell...  20.1 us
    concatenate x1, other arithmetic, local(): hidden = jnp.concatenate([upper, middle, lower], axis=2)  9.7 us
    ppermute x13, waiting for transfers between devices, from_behind(): return lax.ppermute(shard, axis, pairs)  8.39 us
    select_n x6, other arithmetic, neighbour(): return jnp.where(keep, moved, jnp.zeros_like(moved))  4.68 us
    slice x2, local copies, waits for them, and re-layouts, local(): left = neighbour(hidden[:, :, :, width - 4:], 1, offset > 0)  4.5 us
    ppermute x2, local copies, waits for them, and re-layouts, from_behind(): return lax.ppermute(shard, axis, pairs)  4.16 us
  transfers between devices with their start and end apart: 13, of which 3 were waited for; matrix products, arithmetic and copies ran while one was open for 12% of the time, Pallas kernels for 0%

commit v1 on v0

v1 whole, which is shorter than its diff:
```python
import jax
import jax.numpy as jnp
from jax import lax
from jax.sharding import PartitionSpec as P


def band_mask(row_tile, col_tile, start, extent, width, nbins, offsets_total):
    offsets = start + jnp.arange(extent, dtype=jnp.int32)
    row_bins = row_tile * width + offsets
    col_bins = col_tile * width + offsets
    row_ok = (row_bins >= 0) & (row_bins < nbins)
    col_ok = (col_bins >= 0) & (col_bins < nbins)
    gap = jnp.floor_divide(col_bins, width)[None, :] - jnp.floor_divide(row_bins, width)[:, None]
    return row_ok[:, None] & col_ok[None, :] & (gap >= 0) & (gap < offsets_total)


def fetch(trunk, shift_of, n_diag, n_off, offset):
    pairs = []
    for d in range(n_diag):
        for o in range(n_off):
            src = d + shift_of(o)
            if 0 <= src < n_diag and src != d:
                pairs.append((src * n_off + o, d * n_off + o))
    moved = lax.ppermute(trunk, ("diag", "off"), pairs)
    selves = [o for o in range(n_off) if shift_of(o) == 0]
    if not selves:
        return moved
    is_self = jnp.zeros((), jnp.bool_)
    for o in selves:
        is_self = is_self | (offset == o)
    return jnp.where(is_self, trunk, moved)


def local(trunk, w_first, b_first, w_second, b_second):
    samples = trunk.shape[1]
    channels = trunk.shape[2]
    width = trunk.shape[3]
    hidden_width = w_first.shape[0]
    n_off = lax.axis_size("off")
    n_diag = lax.axis_size("diag")
    nbins = n_diag * width
    row_tile = lax.axis_index("diag")
    offset = lax.axis_index("off")
    col_tile = row_tile + offset

    row_prev = fetch(trunk, lambda o: -1, n_diag, n_off, offset)
    row_next = fetch(trunk, lambda o: 1, n_diag, n_off, offset)
    col_prev = fetch(trunk, lambda o: o - 1, n_diag, n_off, offset)
    col_here = fetch(trunk, lambda o: o, n_diag, n_off, offset)
    col_next = fetch(trunk, lambda o: o + 1, n_diag, n_off, offset)

    row_line = jnp.concatenate([row_prev[0], trunk[0], row_next[0]], axis=-1)
    col_line = jnp.concatenate([col_prev[0], col_here[0], col_next[0]], axis=-1)

    extent = width + 12
    inner_size = width + 8
    rows = row_line[:, :, width - 6 : width - 6 + extent]
    cols = col_line[:, :, width - 6 : width - 6 + extent]
    outer_mask = band_mask(row_tile, col_tile, -6, extent, width, nbins, n_off)
    features = jnp.concatenate(
        [
            jnp.broadcast_to(rows[:, :, :, None], (samples, channels, extent, extent)),
            jnp.broadcast_to(cols[:, :, None, :], (samples, channels, extent, extent)),
        ],
        axis=1,
    )
    features = jnp.where(outer_mask[None, None], features, jnp.zeros_like(features))
    pre = jnp.zeros((samples, hidden_width, inner_size, inner_size), jnp.float32)
    for tap_row in range(3):
        for tap_col in range(3):
            window_cells = features[
                :, :, 2 * tap_row : 2 * tap_row + inner_size, 2 * tap_col : 2 * tap_col + inner_size
            ]
            pre = pre + jnp.einsum(
                "hc,bcij->bhij",
                w_first[:, :, tap_row, tap_col],
                window_cells,
                preferred_element_type=jnp.float32,
            )
    inner_mask = band_mask(row_tile, col_tile, -4, inner_size, width, nbins, n_off)
    hidden = jnp.where(
        inner_mask[None, None], jnp.maximum(pre + b_first[None, :, None, None], 0.0), 0.0
    )
    hidden = hidden.astype(jnp.bfloat16)
    result = jnp.zeros((samples, hidden_width, width, width), jnp.float32)
    for tap_row in range(3):
        for tap_col in range(3):
            window_cells = hidden[
                :, :, 4 * tap_row : 4 * tap_row + width, 4 * tap_col : 4 * tap_col + width
            ]
            result = result + jnp.einsum(
                "hk,bkij->bhij",
                w_second[:, :, tap_row, tap_col],
                window_cells,
                preferred_element_type=jnp.float32,
            )
    result = (result + b_second[None, :, None, None]).astype(jnp.bfloat16)
    return result[None, None]


def solution(mesh):
    placed = (P("diag", None, None, None), P(), P(), P(), P())
    return jax.shard_map(
        local,
        mesh=mesh,
        in_specs=placed,
        out_specs=P("diag", "off", None, None, None, None),
        check_vma=False,
    )
```

time: 168 us -> 125 us (0.74)
  the two profiles are of different devices: /device:TPU:193 before, /device:TPU:460 now
where the time goes in v1:
time: 125 us
  matrix products  83 us (66%)
  starting transfers between devices  21.4 us (17%)
  other arithmetic  9.88 us (8%)
  waiting for transfers between devices  6.89 us (6%)
  local copies, waits for them, and re-layouts  3.12 us (2%)
    dot_general x9, matrix products, local(): jnp.einsum('hc,bcij->bhij', w_first[:, :, tap_row, tap_col], window_cells...  66.9 us
    ppermute x5, starting transfers between devices, fetch(): moved = lax.ppermute(trunk, ('diag', 'off'), pairs)  21.4 us
    dot_general x9, matrix products, local(): jnp.einsum('hk,bkij->bhij', w_second[:, :, tap_row, tap_col], window_cell...  16.2 us
    select_n x1, other arithmetic, local(): jnp.where(outer_mask[None, None], features, jnp.zeros_like(features))  7.98 us
    ppermute x5, waiting for transfers between devices, fetch(): moved = lax.ppermute(trunk, ('diag', 'off'), pairs)  6.89 us
  transfers between devices with their start and end apart: 5, of which 1 were waited for; matrix products, arithmetic and copies ran while one was open for 2% of the time, Pallas kernels for 0%

profile of v1, /device:TPU:460, one launch (start us, length us, event | category | flops | bytes accessed | tf_op | source)
XLA Modules:
  0.0 124.5 jit_solution(7016340262396380844)
XLA Ops:
  0.0 2.3 %collective-permute-start.2 = (bf16[1,1,64,128]{3,2,1,0:T(8,128)(2,1)}, bf16[1,1,64,128]{3,2,1,0:T(8,128)(2,1)S(1)}, u32[]{:S(2)}, u32[]{:S(2)}) collective-permute-start(bf16[1,1,64,128]{3,2,1,0:T(8,128)(2,1)} %param.5), channel_id=1, source_target_pairs={{10,2},{19,3},{28,4},{37,5},{46,6},{55,7},{0,8},{18,10},{27,11},{3... | collective-permute-start | bytes 49160 | tf_op jit(solution)/shard_map/ppermute | solution.py:24
  2.3 2.4 %collective-permute-start.1 = (bf16[1,1,64,128]{3,2,1,0:T(8,128)(2,1)}, bf16[1,1,64,128]{3,2,1,0:T(8,128)(2,1)S(1)}, u32[]{:S(2)}, u32[]{:S(2)}) collective-permute-start(bf16[1,1,64,128]{3,2,1,0:T(8,128)(2,1)} %param.5), channel_id=1, source_target_pairs={{8,0},{9,1},{10,2},{11,3},{12,4},{13,5},{14,6},{15,7},{16,8},{17,9... | collective-permute-start | bytes 49160 | tf_op jit(solution)/shard_map/ppermute | solution.py:24
  4.8 3.4 %collective-permute-start = (bf16[1,1,64,128]{3,2,1,0:T(8,128)(2,1)}, bf16[1,1,64,128]{3,2,1,0:T(8,128)(2,1)S(1)}, u32[]{:S(2)}, u32[]{:S(2)}) collective-permute-start(bf16[1,1,64,128]{3,2,1,0:T(8,128)(2,1)} %param.5), channel_id=1, source_target_pairs={{0,8},{1,9},{2,10},{3,11},{4,12},{5,13},{6,14},{7,15},{8,16},{9,17... | collective-permute-start | bytes 49160 | tf_op jit(solution)/shard_map/ppermute | solution.py:24
  8.2 11.3 %collective-permute-start.4 = (bf16[1,1,64,128]{3,2,1,0:T(8,128)(2,1)}, bf16[1,1,64,128]{3,2,1,0:T(8,128)(2,1)S(1)}, u32[]{:S(2)}, u32[]{:S(2)}) collective-permute-start(bf16[1,1,64,128]{3,2,1,0:T(8,128)(2,1)} %param.5), channel_id=1, source_target_pairs={{8,0},{17,1},{26,2},{35,3},{44,4},{53,5},{62,6},{71,7},{16,8},{25,... | collective-permute-start | bytes 49160 | tf_op jit(solution)/shard_map/ppermute | solution.py:24
  19.5 1.9 %collective-permute-start.3 = (bf16[1,1,64,128]{3,2,1,0:T(8,128)(2,1)}, bf16[1,1,64,128]{3,2,1,0:T(8,128)(2,1)S(1)}, u32[]{:S(2)}, u32[]{:S(2)}) collective-permute-start(bf16[1,1,64,128]{3,2,1,0:T(8,128)(2,1)} %param.5), channel_id=1, source_target_pairs={{9,1},{18,2},{27,3},{36,4},{45,5},{54,6},{63,7},{17,9},{26,10},{35... | collective-permute-start | bytes 49160 | tf_op jit(solution)/shard_map/ppermute | solution.py:24
  21.8 6.9 %collective-permute-done.3 = bf16[1,1,64,128]{3,2,1,0:T(8,128)(2,1)S(1)} collective-permute-done((bf16[1,1,64,128]{3,2,1,0:T(8,128)(2,1)}, bf16[1,1,64,128]{3,2,1,0:T(8,128)(2,1)S(1)}, u32[]{:S(2)}, u32[]{:S(2)}) %collective-permute-start.3) | collective-permute-done | bytes 16416 | tf_op jit(solution)/shard_map/ppermute | solution.py:24
  28.6 0.7 select_bitcast_fusion.1
  29.4 0.8 fusion.28
  31.9 8.0 %maximum_select_fusion = bf16[1,128,140,140]{1,3,2,0:T(8,128)(2,1)S(1)} fusion(bf16[1,64,140,140]{1,3,2,0:T(8,128)(2,1)S(1)} %broadcast_in_dim.35, bf16[1,64,140,140]{1,3,2,0:T(8,128)(2,1)S(1)} %broadcast_in_dim.29, pred[140,140]{1,0:T(8,128)(4,1)S(1)} %fusion.24), kind=kLoop, calls=%fused_computation.4 | loop fusion | flops 12544000 | bytes 10054800 | tf_op jit(solution)/shard_map/jit(_where)/select_n | solution.py:67
  39.9 6.1 %fusion.3 = f32[136,136,48]{1,2,0:T(8,128)} fusion(bf16[1,128,140,140]{1,3,2,0:T(8,128)(2,1)S(1)} %maximum_select_fusion, bf16[48,128,3,3]{1,0,3,2:T(8,128)(2,1)S(1)} %copy-done.1), kind=kOutput, calls=%fused_computation.6 | convolution fusion | flops 227278848 | bytes 8298496 | tf_op jit(solution)/shard_map/hc,bcij->bhij/dot_general | solution.py:74
  46.0 6.2 %fusion.4 = f32[136,136,48]{1,2,0:T(8,128)} fusion(bf16[1,128,140,140]{1,3,2,0:T(8,128)(2,1)S(1)} %maximum_select_fusion, bf16[48,128,3,3]{1,0,3,2:T(8,128)(2,1)S(1)} %copy-done.1), kind=kOutput, calls=%fused_computation.8 | convolution fusion | flops 227278848 | bytes 8298496 | tf_op jit(solution)/shard_map/hc,bcij->bhij/dot_general | solution.py:74
  52.2 5.9 %fusion.5 = f32[136,136,48]{1,2,0:T(8,128)} fusion(bf16[1,128,140,140]{1,3,2,0:T(8,128)(2,1)S(1)} %maximum_select_fusion, bf16[48,128,3,3]{1,0,3,2:T(8,128)(2,1)S(1)} %copy-done.1), kind=kOutput, calls=%fused_computation.10 | convolution fusion | flops 227278848 | bytes 8298496 | tf_op jit(solution)/shard_map/hc,bcij->bhij/dot_general | solution.py:74
  58.1 6.2 %fusion.6 = f32[136,136,48]{1,2,0:T(8,128)} fusion(bf16[1,128,140,140]{1,3,2,0:T(8,128)(2,1)S(1)} %maximum_select_fusion, bf16[48,128,3,3]{1,0,3,2:T(8,128)(2,1)S(1)} %copy-done.1), kind=kOutput, calls=%fused_computation.12 | convolution fusion | flops 227278848 | bytes 8298496 | tf_op jit(solution)/shard_map/hc,bcij->bhij/dot_general | solution.py:74
  64.2 6.1 %fusion.7 = f32[136,136,48]{1,2,0:T(8,128)} fusion(bf16[1,128,140,140]{1,3,2,0:T(8,128)(2,1)S(1)} %maximum_select_fusion, bf16[48,128,3,3]{1,0,3,2:T(8,128)(2,1)S(1)} %copy-done.1), kind=kOutput, calls=%fused_computation.14 | convolution fusion | flops 227278848 | bytes 8298496 | tf_op jit(solution)/shard_map/hc,bcij->bhij/dot_general | solution.py:74
  70.3 5.9 %fusion.8 = f32[136,136,48]{1,2,0:T(8,128)} fusion(bf16[1,128,140,140]{1,3,2,0:T(8,128)(2,1)S(1)} %maximum_select_fusion, bf16[48,128,3,3]{1,0,3,2:T(8,128)(2,1)S(1)} %copy-done.1), kind=kOutput, calls=%fused_computation.16 | convolution fusion | flops 227278848 | bytes 8298496 | tf_op jit(solution)/shard_map/hc,bcij->bhij/dot_general | solution.py:74
  76.3 6.3 %fusion.10 = f32[136,136,48]{1,2,0:T(8,128)} fusion(bf16[1,128,140,140]{1,3,2,0:T(8,128)(2,1)S(1)} %maximum_select_fusion, bf16[48,128,3,3]{1,0,3,2:T(8,128)(2,1)S(1)} %copy-done.1), kind=kOutput, calls=%fused_computation.20 | convolution fusion | flops 227278848 | bytes 8298496 | tf_op jit(solution)/shard_map/hc,bcij->bhij/dot_general | solution.py:74
  82.5 6.0 %fusion.11 = f32[136,136,48]{1,2,0:T(8,128)} fusion(bf16[1,128,140,140]{1,3,2,0:T(8,128)(2,1)S(1)} %maximum_select_fusion, bf16[48,128,3,3]{1,0,3,2:T(8,128)(2,1)S(1)} %copy-done.1), kind=kOutput, calls=%fused_computation.22 | convolution fusion | flops 227278848 | bytes 8298496 | tf_op jit(solution)/shard_map/hc,bcij->bhij/dot_general | solution.py:74
  88.5 18.3 %fusion.12 = bf16[1,48,136,136]{3,1,2,0:T(8,128)(2,1)S(1)} fusion(f32[48]{0:T(128)S(1)} %copy-done.3, f32[136,136,48]{1,2,0:T(8,128)} %fusion.3, f32[136,136,48]{1,2,0:T(8,128)} %fusion.4, f32[136,136,48]{1,2,0:T(8,128)} %fusion.5, f32[136,136,48]{1,2,0:T(8,128)} %fusion.6, f32[136,136,48]{1,2,0:T(8,128)} %fusion.7, f32[136,136,48]{1,2,0:T(8,128)} %fusion.8, ...), kind=kOutput, calls=%fused_computation.23 | convolution fusion | flops 237932544 | bytes 34968064 | tf_op jit(solution)/shard_map/hc,bcij->bhij/dot_general | solution.py:74
  108.8 0.7 fusion.17
  110.0 2.3 %fusion.19 = f32[128,128,48]{1,2,0:T(8,128)} fusion(bf16[1,48,136,136]{3,1,2,0:T(8,128)(2,1)S(1)} %fusion.12, bf16[48,48,3,3]{1,0,3,2:T(8,128)(2,1)S(1)} %copy-done), kind=kOutput, calls=%fused_computation.38 | convolution fusion | flops 75497472 | bytes 4730880 | tf_op jit(solution)/shard_map/hk,bkij->bhij/dot_general | solution.py:91
  112.4 2.4 %fusion.20 = f32[128,128,48]{1,2,0:T(8,128)} fusion(bf16[1,48,136,136]{3,1,2,0:T(8,128)(2,1)S(1)} %fusion.12, bf16[48,48,3,3]{1,0,3,2:T(8,128)(2,1)S(1)} %copy-done), kind=kOutput, calls=%fused_computation.40 | convolution fusion | flops 75497472 | bytes 4730880 | tf_op jit(solution)/shard_map/hk,bkij->bhij/dot_general | solution.py:91
  114.8 2.2 %fusion.21 = f32[128,128,48]{1,2,0:T(8,128)} fusion(bf16[1,48,136,136]{3,1,2,0:T(8,128)(2,1)S(1)} %fusion.12, bf16[48,48,3,3]{1,0,3,2:T(8,128)(2,1)S(1)} %copy-done), kind=kOutput, calls=%fused_computation.42 | convolution fusion | flops 75497472 | bytes 4730880 | tf_op jit(solution)/shard_map/hk,bkij->bhij/dot_general | solution.py:91
  117.0 6.0 %fusion.22 = bf16[1,1,1,48,128,128]{5,3,4,2,1,0:T(8,128)(2,1)S(1)} fusion(f32[48]{0:T(128)S(1)} %copy-done.2, bf16[1,48,136,136]{3,1,2,0:T(8,128)(2,1)S(1)} %fusion.12, f32[128,128,48]{1,2,0:T(8,128)S(1)} %fusion.14, f32[128,128,48]{1,2,0:T(8,128)S(1)} %fusion.15, f32[128,128,48]{1,2,0:T(8,128)S(1)} %fusion.16, f32[128,128,48]{1,2,0:T(8,128)S(1)} %fusion.17, ...), kind=kOutput, calls=%fused_computation.43 | convolution fusion | flops 83361792 | bytes 28324352 | tf_op jit(solution)/shard_map/hk,bkij->bhij/dot_general | solution.py:91
  123.0 1.6 %copy.8 = bf16[1,1,1,48,128,128]{5,4,3,2,1,0:T(8,128)(2,1)} copy(bf16[1,1,1,48,128,128]{5,3,4,2,1,0:T(8,128)(2,1)S(1)} %fusion.22) | data formatting | bytes 3145728 | tf_op jit(solution)/shard_map/broadcast_in_dim | solution.py:98
  (27 shorter events, 4.5 us)
Async XLA Ops:
  0.0 21.8 %collective-permute-start.2 = (bf16[1,1,64,128]{3,2,1,0:T(8,128)(2,1)}, bf16[1,1,64,128]{3,2,1,0:T(8,128)(2,1)S(1)}, u32[]{:S(2)}, u32[]{:S(2)}) collective-permute-start(bf16[1,1,64,128]{3,2,1,0:T(8,128)(2,1)} %param.5), channel_id=1, source_target_pairs={{10,2},{19,3},{28,4},{37,5},{46,6},{55,7},{0,8},{18,10},{27,11},{3... | collective-permute-start | bytes 49160 | tf_op jit(solution)/shard_map/ppermute | solution.py:24
  2.3 27.0 %collective-permute-start.1 = (bf16[1,1,64,128]{3,2,1,0:T(8,128)(2,1)}, bf16[1,1,64,128]{3,2,1,0:T(8,128)(2,1)S(1)}, u32[]{:S(2)}, u32[]{:S(2)}) collective-permute-start(bf16[1,1,64,128]{3,2,1,0:T(8,128)(2,1)} %param.5), channel_id=1, source_target_pairs={{8,0},{9,1},{10,2},{11,3},{12,4},{13,5},{14,6},{15,7},{16,8},{17,9... | collective-permute-start | bytes 49160 | tf_op jit(solution)/shard_map/ppermute | solution.py:24
  4.8 24.6 %collective-permute-start = (bf16[1,1,64,128]{3,2,1,0:T(8,128)(2,1)}, bf16[1,1,64,128]{3,2,1,0:T(8,128)(2,1)S(1)}, u32[]{:S(2)}, u32[]{:S(2)}) collective-permute-start(bf16[1,1,64,128]{3,2,1,0:T(8,128)(2,1)} %param.5), channel_id=1, source_target_pairs={{0,8},{1,9},{2,10},{3,11},{4,12},{5,13},{6,14},{7,15},{8,16},{9,17... | collective-permute-start | bytes 49160 | tf_op jit(solution)/shard_map/ppermute | solution.py:24
  8.2 22.1 %collective-permute-start.4 = (bf16[1,1,64,128]{3,2,1,0:T(8,128)(2,1)}, bf16[1,1,64,128]{3,2,1,0:T(8,128)(2,1)S(1)}, u32[]{:S(2)}, u32[]{:S(2)}) collective-permute-start(bf16[1,1,64,128]{3,2,1,0:T(8,128)(2,1)} %param.5), channel_id=1, source_target_pairs={{8,0},{17,1},{26,2},{35,3},{44,4},{53,5},{62,6},{71,7},{16,8},{25,... | collective-permute-start | bytes 49160 | tf_op jit(solution)/shard_map/ppermute | solution.py:24
  19.5 9.1 %collective-permute-start.3 = (bf16[1,1,64,128]{3,2,1,0:T(8,128)(2,1)}, bf16[1,1,64,128]{3,2,1,0:T(8,128)(2,1)S(1)}, u32[]{:S(2)}, u32[]{:S(2)}) collective-permute-start(bf16[1,1,64,128]{3,2,1,0:T(8,128)(2,1)} %param.5), channel_id=1, source_target_pairs={{9,1},{18,2},{27,3},{36,4},{45,5},{54,6},{63,7},{17,9},{26,10},{35... | collective-permute-start | bytes 49160 | tf_op jit(solution)/shard_map/ppermute | solution.py:24
  31.9 8.0 %copy-start.1 = (bf16[48,128,3,3]{1,0,3,2:T(8,128)(2,1)S(1)}, bf16[48,128,3,3]{1,0,3,2:T(8,128)(2,1)}, u32[]{:S(2)}) copy-start(bf16[48,128,3,3]{1,0,3,2:T(8,128)(2,1)} %param.6) | copy-start | bytes 331780
  82.5 6.0 %copy-start.3 = (f32[48]{0:T(128)S(1)}, f32[48]{0:T(128)}, u32[]{:S(2)}) copy-start(f32[48]{0:T(128)} %param.7) | copy-start | bytes 580
  88.5 18.3 %copy-start = (bf16[48,48,3,3]{1,0,3,2:T(8,128)(2,1)S(1)}, bf16[48,48,3,3]{1,0,3,2:T(8,128)(2,1)}, u32[]{:S(2)}) copy-start(bf16[48,48,3,3]{1,0,3,2:T(8,128)(2,1)} %param.8) | copy-start | bytes 124420
  112.4 4.6 %copy-start.2 = (f32[48]{0:T(128)S(1)}, f32[48]{0:T(128)}, u32[]{:S(2)}) copy-start(f32[48]{0:T(128)} %param.9) | copy-start | bytes 580

commit v2 on v1

--- a/solution.py
+++ b/solution.py
@@ -31,6 +31,53 @@
     return jnp.where(is_self, trunk, moved)
 
 
+def block_indicator(tile, start, extent, width, nbins):
+    bins = tile * width + start + jnp.arange(extent, dtype=jnp.int32)
+    ok = (bins >= 0) & (bins < nbins)
+    block = jnp.floor_divide(bins, width) - tile + 1
+    return (ok[None, :] & (block[None, :] == jnp.arange(3, dtype=jnp.int32)[:, None])).astype(jnp.float32)
+
+
+def split_bf16(value):
+    high = value.astype(jnp.bfloat16)
+    low = (value - high.astype(jnp.float32)).astype(jnp.bfloat16)
+    return high, low
+
+
+def first_conv(rows, cols, w_first, row_tile, col_tile, offset, width, nbins, n_off):
+    channels = rows.shape[0]
+    extent = rows.shape[1]
+    size = extent - 4
+    a_ind = block_indicator(row_tile, -6, extent, width, nbins)
+    b_ind = block_indicator(col_tile, -6, extent, width, nbins)
+    steps = jnp.arange(3, dtype=jnp.int32)
+    gap = offset + steps[None, :] - steps[:, None]
+    g = ((gap >= 0) & (gap < n_off)).astype(jnp.float32)
+    r = jnp.einsum("hcuv,ci->uvhi", w_first[:, :channels], rows, preferred_element_type=jnp.float32)
+    c = jnp.einsum("hcuv,cj->uvhj", w_first[:, channels:], cols, preferred_element_type=jnp.float32)
+    p_row = sum(
+        a_ind[None, None, :, 2 * u : 2 * u + size] * r[u][:, :, None, 2 * u : 2 * u + size]
+        for u in range(3)
+    )
+    b_sel = jnp.einsum("ab,bj->aj", g, b_ind)
+    q_col = jnp.stack([b_sel[:, 2 * v : 2 * v + size] for v in range(3)], axis=1)
+    p_col = sum(
+        b_ind[None, None, :, 2 * v : 2 * v + size] * c[:, v][:, :, None, 2 * v : 2 * v + size]
+        for v in range(3)
+    )
+    a_sel = jnp.einsum("ab,ai->bi", g, a_ind)
+    q_row = jnp.stack([a_sel[:, 2 * u : 2 * u + size] for u in range(3)], axis=1)
+    p_row_hi, p_row_lo = split_bf16(p_row)
+    p_col_hi, p_col_lo = split_bf16(p_col)
+    q_col = q_col.astype(jnp.bfloat16)
+    q_row = q_row.astype(jnp.bfloat16)
+    term_row = jnp.einsum("vhai,avj->hij", p_row_hi, q_col, preferred_element_type=jnp.float32)
+    term_row = term_row + jnp.einsum("vhai,avj->hij", p_row_lo, q_col, preferred_element_type=jnp.float32)
+    term_col = jnp.einsum("bui,uhbj->hij", q_row, p_col_hi, preferred_element_type=jnp.float32)
+    term_col = term_col + jnp.einsum("bui,uhbj->hij", q_row, p_col_lo, preferred_element_type=jnp.float32)
+    return term_row + term_col
+
+
 def local(trunk, w_first, b_first, w_second, b_second):
     samples = trunk.shape[1]
     channels = trunk.shape[2]
@@ -56,27 +103,8 @@
     inner_size = width + 8
     rows = row_line[:, :, width - 6 : width - 6 + extent]
     cols = col_line[:, :, width - 6 : width - 6 + extent]
-    outer_mask = band_mask(row_tile, col_tile, -6, extent, width, nbins, n_off)
-    features = jnp.concatenate(
-        [
-            jnp.broadcast_to(rows[:, :, :, None], (samples, channels, extent, extent)),
-            jnp.broadcast_to(cols[:, :, None, :], (samples, channels, extent, extent)),
-        ],
-        axis=1,
-    )
-    features = jnp.where(outer_mask[None, None], features, jnp.zeros_like(features))
-    pre = jnp.zeros((samples, hidden_width, inner_size, inner_size), jnp.float32)
-    for tap_row in range(3):
-        for tap_col in range(3):
-            window_cells = features[
-                :, :, 2 * tap_row : 2 * tap_row + inner_size, 2 * tap_col : 2 * tap_col + inner_size
-            ]
-            pre = pre + jnp.einsum(
-                "hc,bcij->bhij",
-                w_first[:, :, tap_row, tap_col],
-                window_cells,
-                preferred_element_type=jnp.float32,
-            )
+    pre = first_conv(rows[0], cols[0], w_first, row_tile, col_tile, offset, width, nbins, n_off)
+    pre = pre[None]
     inner_mask = band_mask(row_tile, col_tile, -4, inner_size, width, nbins, n_off)
     hidden = jnp.where(
         inner_mask[None, None], jnp.maximum(pre + b_first[None, :, None, None], 0.0), 0.0

time: 125 us -> 61.4 us (0.49)
  the two profiles are of different devices: /device:TPU:460 before, /device:TPU:472 now
where the time goes in v2:
time: 61.4 us; the launch traced here: 61 us
  matrix products  26.2 us (43%)
  starting transfers between devices  24.2 us (39%)
  local copies, waits for them, and re-layouts  9.99 us (16%)
    ppermute x5, starting transfers between devices, fetch(): moved = lax.ppermute(trunk, ('diag', 'off'), pairs)  24.2 us
    dot_general x9, matrix products, local(): jnp.einsum('hk,bkij->bhij', w_second[:, :, tap_row, tap_col], window_cell...  18.6 us
    another operation x1, local copies, waits for them, and re-layouts  5.62 us
    broadcast_in_dim x1, local copies, waits for them, and re-layouts, local(): return result[None, None]  2.96 us
    dot_general x1, matrix products, first_conv(): jnp.einsum('bui,uhbj->hij', q_row, p_col_lo, preferred_element_type=jnp.f...  2.39 us
  transfers between devices with their start and end apart: 5, of which 0 were waited for; matrix products, arithmetic and copies ran while one was open for 8% of the time, Pallas kernels for 0%

profile of v2, /device:TPU:472, one launch (start us, length us, event | category | flops | bytes accessed | tf_op | source)
XLA Modules:
  0.0 61.0 jit_solution(11439650230046389375)
XLA Ops:
  0.0 4.4 %collective-permute-start.2 = (bf16[1,1,64,128]{3,2,1,0:T(8,128)(2,1)}, bf16[1,1,64,128]{3,2,1,0:T(8,128)(2,1)S(1)}, u32[]{:S(2)}, u32[]{:S(2)}) collective-permute-start(bf16[1,1,64,128]{3,2,1,0:T(8,128)(2,1)} %param.5), channel_id=1, source_target_pairs={{10,2},{19,3},{28,4},{37,5},{46,6},{55,7},{0,8},{18,10},{27,11},{3... | collective-permute-start | bytes 49160 | tf_op jit(solution)/shard_map/ppermute | solution.py:24
  4.4 2.7 %collective-permute-start.1 = (bf16[1,1,64,128]{3,2,1,0:T(8,128)(2,1)}, bf16[1,1,64,128]{3,2,1,0:T(8,128)(2,1)S(1)}, u32[]{:S(2)}, u32[]{:S(2)}) collective-permute-start(bf16[1,1,64,128]{3,2,1,0:T(8,128)(2,1)} %param.5), channel_id=1, source_target_pairs={{8,0},{9,1},{10,2},{11,3},{12,4},{13,5},{14,6},{15,7},{16,8},{17,9... | collective-permute-start | bytes 49160 | tf_op jit(solution)/shard_map/ppermute | solution.py:24
  7.2 3.1 %collective-permute-start = (bf16[1,1,64,128]{3,2,1,0:T(8,128)(2,1)}, bf16[1,1,64,128]{3,2,1,0:T(8,128)(2,1)S(1)}, u32[]{:S(2)}, u32[]{:S(2)}) collective-permute-start(bf16[1,1,64,128]{3,2,1,0:T(8,128)(2,1)} %param.5), channel_id=1, source_target_pairs={{0,8},{1,9},{2,10},{3,11},{4,12},{5,13},{6,14},{7,15},{8,16},{9,17... | collective-permute-start | bytes 49160 | tf_op jit(solution)/shard_map/ppermute | solution.py:24
  10.3 4.7 %collective-permute-start.4 = (bf16[1,1,64,128]{3,2,1,0:T(8,128)(2,1)}, bf16[1,1,64,128]{3,2,1,0:T(8,128)(2,1)S(1)}, u32[]{:S(2)}, u32[]{:S(2)}) collective-permute-start(bf16[1,1,64,128]{3,2,1,0:T(8,128)(2,1)} %param.5), channel_id=1, source_target_pairs={{8,0},{17,1},{26,2},{35,3},{44,4},{53,5},{62,6},{71,7},{16,8},{25,... | collective-permute-start | bytes 49160 | tf_op jit(solution)/shard_map/ppermute | solution.py:24
  15.0 9.2 %collective-permute-start.3 = (bf16[1,1,64,128]{3,2,1,0:T(8,128)(2,1)}, bf16[1,1,64,128]{3,2,1,0:T(8,128)(2,1)S(1)}, u32[]{:S(2)}, u32[]{:S(2)}) collective-permute-start(bf16[1,1,64,128]{3,2,1,0:T(8,128)(2,1)} %param.5), channel_id=1, source_target_pairs={{9,1},{18,2},{27,3},{36,4},{45,5},{54,6},{63,7},{17,9},{26,10},{35... | collective-permute-start | bytes 49160 | tf_op jit(solution)/shard_map/ppermute | solution.py:24
  24.4 0.2 convolution_convert_fusion
  24.5 0.1 convolution_convert_fusion.1
  25.2 1.2 %convolution_bitcast_fusion.1 = f32[3,3,48,140]{3,2,1,0:T(8,128)S(1)} fusion(bf16[48,128,3,3]{1,0,3,2:T(8,128)(2,1)} %param.6, bf16[1,64,128]{2,1,0:T(8,128)(2,1)S(1)} %bitcast.177, bf16[1,64,128]{2,1,0:T(8,128)(2,1)} %bitcast.175, bf16[1,64,128]{2,1,0:T(8,128)(2,1)S(1)} %bitcast.178), kind=kOutput, calls=%fused_computation.38 | convolution fusion | flops 7795200 | bytes 401664 | tf_op jit(solution)/shard_map/hcuv,ci->uvhi/dot_general | solution.py:56
  26.9 1.1 %fusion.28 = f32[48,136,136,1]{2,1,3,0:T(8,128)S(1)} fusion(f32[3,48,136]{2,0,1:T(4,128)S(1)} %copy.8, f32[3,136]{1,0:T(4,128)S(1)} %get-tuple-element.23, f32[3,48,136]{2,0,1:T(4,128)S(1)} %copy.7, f32[3,136]{1,0:T(4,128)S(1)} %get-tuple-element.24, f32[3,48,136]{2,0,1:T(4,128)S(1)} %copy.6, f32[3,136]{1,0:T(4,128)S(1)} %get-tuple-element.22, ...), kind=kOutput, calls=%fused_computation.47 | convolution fusion | flops 16509312 | bytes 3793584 | tf_op jit(solution)/shard_map/vhai,avj->hij/dot_general | solution.py:75
  28.1 1.1 %fusion.73 = f32[48,136,136,1]{2,1,3,0:T(8,128)S(1)} fusion(bf16[3,3,136]{2,0,1:T(4,128)(2,1)S(1)} %pad_maximum_fusion.6, f32[3,48,136]{2,0,1:T(4,128)S(1)} %copy.8, f32[3,136]{1,0:T(4,128)S(1)} %get-tuple-element.23, f32[3,48,136]{2,0,1:T(4,128)S(1)} %copy.7, f32[3,136]{1,0:T(4,128)S(1)} %get-tuple-element.24, f32[3,48,136]{2,0,1:T(4,128)S(1)} %copy.6, ...), kind=kOutput, calls=%fused_computation.106 | convolution fusion | flops 16333056 | bytes 3793584 | tf_op jit(solution)/shard_map/vhai,avj->hij/dot_general | solution.py:74
  29.3 0.3 convolution_bitcast_fusion
  30.2 1.1 %fusion.70 = f32[48,136,136,1]{1,2,3,0:T(8,128)S(1)} fusion(bf16[3,3,136]{2,0,1:T(4,128)(2,1)S(1)} %pad_maximum_fusion.7, f32[3,48,136]{2,0,1:T(4,128)S(1)} %copy.13, f32[3,136]{1,0:T(4,128)S(1)} %get-tuple-element.26, f32[3,48,136]{2,0,1:T(4,128)S(1)} %copy.12, f32[3,136]{1,0:T(4,128)S(1)} %get-tuple-element.27, f32[3,48,136]{2,0,1:T(4,128)S(1)} %copy.11, ...), kind=kOutput, calls=%fused_computation.103 | convolution fusion | flops 16333056 | bytes 3793584 | tf_op jit(solution)/shard_map/bui,uhbj->hij/dot_general | solution.py:76
  31.4 2.4 %fusion.4 = bf16[1,48,136,136]{3,2,1,0:T(8,128)(2,1)S(1)} fusion(f32[48,136,136,1]{1,2,3,0:T(8,128)S(1)} %fusion.70, f32[48,136,136,1]{2,1,3,0:T(8,128)S(1)} %fusion.28, f32[48,136,136,1]{2,1,3,0:T(8,128)S(1)} %fusion.73, f32[48]{0:T(128)S(1)} %copy-done.5, pred[136,136]{1,0:T(8,128)(4,1)S(1)} %fusion.42, f32[3,48,136]{2,0,1:T(4,128)S(1)} %copy.13, ...), kind=kOutput, calls=%fused_computation.7 | convolution fusion | flops 22723968 | bytes 12690352 | tf_op jit(solution)/shard_map/bui,uhbj->hij/dot_general | solution.py:77
  33.8 5.6 %slice_bitcast_fusion.7 = (bf16[48,128,128]{2,1,0:T(8,128)(2,1)S(1)}, bf16[48,128,128]{2,1,0:T(8,128)(2,1)S(1)}, bf16[48,128,128]{2,1,0:T(8,128)(2,1)S(1)}, bf16...) fusion(bf16[1,48,136,136]{3,2,1,0:T(8,128)(2,1)S(1)} %fusion.4), kind=kLoop, calls=%fused_computation.17 | loop fusion | bytes 28311552 | tf_op jit(solution)/shard_map/reshape.4
  39.4 1.4 %fusion.19 = f32[128,128,48]{1,2,0:T(8,128)S(1)} fusion(bf16[48,128,128]{2,1,0:T(8,128)(2,1)S(1)} %get-tuple-element.5, bf16[48,48,3,3]{1,0,3,2:T(8,128)(2,1)S(1)} %copy-done.3), kind=kOutput, calls=%fused_computation.32 | convolution fusion | flops 75497472 | bytes 4730880 | tf_op jit(solution)/shard_map/hk,bkij->bhij/dot_general | solution.py:119
  40.8 1.4 %fusion.7 = f32[128,128,48]{1,2,0:T(8,128)S(1)} fusion(bf16[48,128,128]{2,1,0:T(8,128)(2,1)S(1)} %get-tuple-element.7, bf16[48,48,3,3]{1,0,3,2:T(8,128)(2,1)S(1)} %copy-done.3), kind=kOutput, calls=%fused_computation.20 | convolution fusion | flops 75497472 | bytes 4730880 | tf_op jit(solution)/shard_map/hk,bkij->bhij/dot_general | solution.py:119
  42.2 1.4 %fusion.9 = f32[128,128,48]{1,2,0:T(8,128)S(1)} fusion(bf16[48,128,128]{2,1,0:T(8,128)(2,1)S(1)} %get-tuple-element.8, bf16[48,48,3,3]{1,0,3,2:T(8,128)(2,1)S(1)} %copy-done.3), kind=kOutput, calls=%fused_computation.22 | convolution fusion | flops 75497472 | bytes 4730880 | tf_op jit(solution)/shard_map/hk,bkij->bhij/dot_general | solution.py:119
  43.6 1.4 %fusion.11 = f32[128,128,48]{1,2,0:T(8,128)S(1)} fusion(bf16[48,128,128]{2,1,0:T(8,128)(2,1)S(1)} %get-tuple-element.9, bf16[48,48,3,3]{1,0,3,2:T(8,128)(2,1)S(1)} %copy-done.3), kind=kOutput, calls=%fused_computation.24 | convolution fusion | flops 75497472 | bytes 4730880 | tf_op jit(solution)/shard_map/hk,bkij->bhij/dot_general | solution.py:119
  45.0 1.4 %fusion.13 = f32[128,128,48]{1,2,0:T(8,128)S(1)} fusion(bf16[48,128,128]{2,1,0:T(8,128)(2,1)S(1)} %get-tuple-element.10, bf16[48,48,3,3]{1,0,3,2:T(8,128)(2,1)S(1)} %copy-done.3), kind=kOutput, calls=%fused_computation.26 | convolution fusion | flops 75497472 | bytes 4730880 | tf_op jit(solution)/shard_map/hk,bkij->bhij/dot_general | solution.py:119
  46.4 1.4 %fusion.15 = f32[128,128,48]{1,2,0:T(8,128)S(1)} fusion(bf16[48,128,128]{2,1,0:T(8,128)(2,1)S(1)} %get-tuple-element.11, bf16[48,48,3,3]{1,0,3,2:T(8,128)(2,1)S(1)} %copy-done.3), kind=kOutput, calls=%fused_computation.28 | convolution fusion | flops 75497472 | bytes 4730880 | tf_op jit(solution)/shard_map/hk,bkij->bhij/dot_general | solution.py:119
  47.8 1.4 %fusion.17 = f32[128,128,48]{1,2,0:T(8,128)S(1)} fusion(bf16[48,128,128]{2,1,0:T(8,128)(2,1)S(1)} %copy-done.1, bf16[48,48,3,3]{1,0,3,2:T(8,128)(2,1)S(1)} %copy-done.3), kind=kOutput, calls=%fused_computation.30 | convolution fusion | flops 75497472 | bytes 4730880 | tf_op jit(solution)/shard_map/hk,bkij->bhij/dot_general | solution.py:119
  49.2 3.0 %fusion.21 = f32[128,128,48]{1,2,0:T(8,128)} fusion(bf16[48,128,128]{2,1,0:T(8,128)(2,1)S(1)} %copy-done, bf16[48,48,3,3]{1,0,3,2:T(8,128)(2,1)S(1)} %copy-done.3), kind=kOutput, calls=%fused_computation.34 | convolution fusion | flops 75497472 | bytes 4730880 | tf_op jit(solution)/shard_map/hk,bkij->bhij/dot_general | solution.py:119
  52.3 5.8 %fusion.23 = bf16[1,1,1,48,128,128]{5,3,4,2,1,0:T(8,128)(2,1)} fusion(f32[48]{0:T(128)S(1)} %copy-done.6, bf16[48,128,128]{2,1,0:T(8,128)(2,1)S(1)} %get-tuple-element.6, f32[128,128,48]{1,2,0:T(8,128)S(1)} %fusion.7, f32[128,128,48]{1,2,0:T(8,128)S(1)} %fusion.9, f32[128,128,48]{1,2,0:T(8,128)S(1)} %fusion.11, f32[128,128,48]{1,2,0:T(8,128)S(1)} %fusion.13, ...), kind=kOutput, calls=%fused_computation.36 | convolution fusion | flops 83361792 | bytes 28324352 | tf_op jit(solution)/shard_map/hk,bkij->bhij/dot_general | solution.py:119
  58.1 3.0 %copy.27 = bf16[1,1,1,48,128,128]{5,4,3,2,1,0:T(8,128)(2,1)} copy(bf16[1,1,1,48,128,128]{5,3,4,2,1,0:T(8,128)(2,1)} %fusion.23) | data formatting | bytes 3145728 | tf_op jit(solution)/shard_map/broadcast_in_dim | solution.py:126
  (48 shorter events, 1.7 us)
Async XLA Ops:
  0.0 29.3 %collective-permute-start.2 = (bf16[1,1,64,128]{3,2,1,0:T(8,128)(2,1)}, bf16[1,1,64,128]{3,2,1,0:T(8,128)(2,1)S(1)}, u32[]{:S(2)}, u32[]{:S(2)}) collective-permute-start(bf16[1,1,64,128]{3,2,1,0:T(8,128)(2,1)} %param.5), channel_id=1, source_target_pairs={{10,2},{19,3},{28,4},{37,5},{46,6},{55,7},{0,8},{18,10},{27,11},{3... | collective-permute-start | bytes 49160 | tf_op jit(solution)/shard_map/ppermute | solution.py:24
  4.4 20.7 %collective-permute-start.1 = (bf16[1,1,64,128]{3,2,1,0:T(8,128)(2,1)}, bf16[1,1,64,128]{3,2,1,0:T(8,128)(2,1)S(1)}, u32[]{:S(2)}, u32[]{:S(2)}) collective-permute-start(bf16[1,1,64,128]{3,2,1,0:T(8,128)(2,1)} %param.5), channel_id=1, source_target_pairs={{8,0},{9,1},{10,2},{11,3},{12,4},{13,5},{14,6},{15,7},{16,8},{17,9... | collective-permute-start | bytes 49160 | tf_op jit(solution)/shard_map/ppermute | solution.py:24
  7.2 18.0 %collective-permute-start = (bf16[1,1,64,128]{3,2,1,0:T(8,128)(2,1)}, bf16[1,1,64,128]{3,2,1,0:T(8,128)(2,1)S(1)}, u32[]{:S(2)}, u32[]{:S(2)}) collective-permute-start(bf16[1,1,64,128]{3,2,1,0:T(8,128)(2,1)} %param.5), channel_id=1, source_target_pairs={{0,8},{1,9},{2,10},{3,11},{4,12},{5,13},{6,14},{7,15},{8,16},{9,17... | collective-permute-start | bytes 49160 | tf_op jit(solution)/shard_map/ppermute | solution.py:24
  10.3 19.0 %collective-permute-start.4 = (bf16[1,1,64,128]{3,2,1,0:T(8,128)(2,1)}, bf16[1,1,64,128]{3,2,1,0:T(8,128)(2,1)S(1)}, u32[]{:S(2)}, u32[]{:S(2)}) collective-permute-start(bf16[1,1,64,128]{3,2,1,0:T(8,128)(2,1)} %param.5), channel_id=1, source_target_pairs={{8,0},{17,1},{26,2},{35,3},{44,4},{53,5},{62,6},{71,7},{16,8},{25,... | collective-permute-start | bytes 49160 | tf_op jit(solution)/shard_map/ppermute | solution.py:24
  15.0 14.3 %collective-permute-start.3 = (bf16[1,1,64,128]{3,2,1,0:T(8,128)(2,1)}, bf16[1,1,64,128]{3,2,1,0:T(8,128)(2,1)S(1)}, u32[]{:S(2)}, u32[]{:S(2)}) collective-permute-start(bf16[1,1,64,128]{3,2,1,0:T(8,128)(2,1)} %param.5), channel_id=1, source_target_pairs={{9,1},{18,2},{27,3},{36,4},{45,5},{54,6},{63,7},{17,9},{26,10},{35... | collective-permute-start | bytes 49160 | tf_op jit(solution)/shard_map/ppermute | solution.py:24
  28.1 1.2 %copy-start.4 = (bf16[1,1,64,128]{3,2,1,0:T(8,128)(2,1)S(1)}, bf16[1,1,64,128]{3,2,1,0:T(8,128)(2,1)}, u32[]{:S(2)}) copy-start(bf16[1,1,64,128]{3,2,1,0:T(8,128)(2,1)} %param.5) | copy-start | bytes 49156
  28.1 1.2 %copy-start.2 = (bf16[48,128,3,3]{1,0,3,2:T(8,128)(2,1)S(1)}, bf16[48,128,3,3]{1,0,3,2:T(8,128)(2,1)}, u32[]{:S(2)}) copy-start(bf16[48,128,3,3]{1,0,3,2:T(8,128)(2,1)} %param.6) | copy-start | bytes 331780
  30.2 1.2 %copy-start.5 = (f32[48]{0:T(128)S(1)}, f32[48]{0:T(128)}, u32[]{:S(2)}) copy-start(f32[48]{0:T(128)} %param.7) | copy-start | bytes 580
  33.8 5.6 %copy-start.3 = (bf16[48,48,3,3]{1,0,3,2:T(8,128)(2,1)S(1)}, bf16[48,48,3,3]{1,0,3,2:T(8,128)(2,1)}, u32[]{:S(2)}) copy-start(bf16[48,48,3,3]{1,0,3,2:T(8,128)(2,1)} %param.8) | copy-start | bytes 124420
  46.4 1.4 %copy-start.1 = (bf16[48,128,128]{2,1,0:T(8,128)(2,1)S(1)}, bf16[48,128,128]{2,1,0:T(8,128)(2,1)}, u32[]{:S(2)}) copy-start(bf16[48,128,128]{2,1,0:T(8,128)(2,1)} %get-tuple-element.12) | copy-start | bytes 4718596
  47.8 1.4 %copy-start = (bf16[48,128,128]{2,1,0:T(8,128)(2,1)S(1)}, bf16[48,128,128]{2,1,0:T(8,128)(2,1)}, u32[]{:S(2)}) copy-start(bf16[48,128,128]{2,1,0:T(8,128)(2,1)} %get-tuple-element.13) | copy-start | bytes 4718596
  49.2 3.1 %copy-start.6 = (f32[48]{0:T(128)S(1)}, f32[48]{0:T(128)}, u32[]{:S(2)}) copy-start(f32[48]{0:T(128)} %param.9) | copy-start | bytes 580

commit v3 on v2

--- a/solution.py
+++ b/solution.py
@@ -39,9 +39,9 @@
 
 
 def split_bf16(value):
-    high = value.astype(jnp.bfloat16)
-    low = (value - high.astype(jnp.float32)).astype(jnp.bfloat16)
-    return high, low
+    high = lax.reduce_precision(value, exponent_bits=8, mantissa_bits=7)
+    low = value - high
+    return high.astype(jnp.bfloat16), low.astype(jnp.bfloat16)
 
 
 def first_conv(rows, cols, w_first, row_tile, col_tile, offset, width, nbins, n_off):

time: 61.4 us -> 61.4 us (level)
  no operation moved by 1% of the time
where the time goes in v3:
time: 61.4 us; the launch traced here: 61 us
  matrix products  26.1 us (43%)
  starting transfers between devices  24.2 us (39%)
  local copies, waits for them, and re-layouts  9.99 us (16%)
    ppermute x5, starting transfers between devices, fetch(): moved = lax.ppermute(trunk, ('diag', 'off'), pairs)  24.2 us
    dot_general x9, matrix products, local(): jnp.einsum('hk,bkij->bhij', w_second[:, :, tap_row, tap_col], window_cell...  18.6 us
    another operation x1, local copies, waits for them, and re-layouts  5.62 us
    broadcast_in_dim x1, local copies, waits for them, and re-layouts, local(): return result[None, None]  2.96 us
    dot_general x1, matrix products, first_conv(): jnp.einsum('bui,uhbj->hij', q_row, p_col_lo, preferred_element_type=jnp.f...  2.37 us
  transfers between devices with their start and end apart: 5, of which 0 were waited for; matrix products, arithmetic and copies ran while one was open for 8% of the time, Pallas kernels for 0%

profile of v3, /device:TPU:472, one launch (start us, length us, event | category | flops | bytes accessed | tf_op | source)
XLA Modules:
  0.0 61.0 jit_solution(17999900610745663911)
XLA Ops:
  0.0 4.4 %collective-permute-start.2 = (bf16[1,1,64,128]{3,2,1,0:T(8,128)(2,1)}, bf16[1,1,64,128]{3,2,1,0:T(8,128)(2,1)S(1)}, u32[]{:S(2)}, u32[]{:S(2)}) collective-permute-start(bf16[1,1,64,128]{3,2,1,0:T(8,128)(2,1)} %param.5), channel_id=1, source_target_pairs={{10,2},{19,3},{28,4},{37,5},{46,6},{55,7},{0,8},{18,10},{27,11},{3... | collective-permute-start | bytes 49160 | tf_op jit(solution)/shard_map/ppermute | solution.py:24
  4.4 2.7 %collective-permute-start.1 = (bf16[1,1,64,128]{3,2,1,0:T(8,128)(2,1)}, bf16[1,1,64,128]{3,2,1,0:T(8,128)(2,1)S(1)}, u32[]{:S(2)}, u32[]{:S(2)}) collective-permute-start(bf16[1,1,64,128]{3,2,1,0:T(8,128)(2,1)} %param.5), channel_id=1, source_target_pairs={{8,0},{9,1},{10,2},{11,3},{12,4},{13,5},{14,6},{15,7},{16,8},{17,9... | collective-permute-start | bytes 49160 | tf_op jit(solution)/shard_map/ppermute | solution.py:24
  7.2 3.1 %collective-permute-start = (bf16[1,1,64,128]{3,2,1,0:T(8,128)(2,1)}, bf16[1,1,64,128]{3,2,1,0:T(8,128)(2,1)S(1)}, u32[]{:S(2)}, u32[]{:S(2)}) collective-permute-start(bf16[1,1,64,128]{3,2,1,0:T(8,128)(2,1)} %param.5), channel_id=1, source_target_pairs={{0,8},{1,9},{2,10},{3,11},{4,12},{5,13},{6,14},{7,15},{8,16},{9,17... | collective-permute-start | bytes 49160 | tf_op jit(solution)/shard_map/ppermute | solution.py:24
  10.3 4.7 %collective-permute-start.4 = (bf16[1,1,64,128]{3,2,1,0:T(8,128)(2,1)}, bf16[1,1,64,128]{3,2,1,0:T(8,128)(2,1)S(1)}, u32[]{:S(2)}, u32[]{:S(2)}) collective-permute-start(bf16[1,1,64,128]{3,2,1,0:T(8,128)(2,1)} %param.5), channel_id=1, source_target_pairs={{8,0},{17,1},{26,2},{35,3},{44,4},{53,5},{62,6},{71,7},{16,8},{25,... | collective-permute-start | bytes 49160 | tf_op jit(solution)/shard_map/ppermute | solution.py:24
  15.0 9.2 %collective-permute-start.3 = (bf16[1,1,64,128]{3,2,1,0:T(8,128)(2,1)}, bf16[1,1,64,128]{3,2,1,0:T(8,128)(2,1)S(1)}, u32[]{:S(2)}, u32[]{:S(2)}) collective-permute-start(bf16[1,1,64,128]{3,2,1,0:T(8,128)(2,1)} %param.5), channel_id=1, source_target_pairs={{9,1},{18,2},{27,3},{36,4},{45,5},{54,6},{63,7},{17,9},{26,10},{35... | collective-permute-start | bytes 49160 | tf_op jit(solution)/shard_map/ppermute | solution.py:24
  24.4 0.2 convolution_convert_fusion
  24.5 0.1 convolution_convert_fusion.1
  25.2 1.2 %convolution_bitcast_fusion.1 = f32[3,3,48,140]{3,2,1,0:T(8,128)S(1)} fusion(bf16[48,128,3,3]{1,0,3,2:T(8,128)(2,1)} %param.6, bf16[1,64,128]{2,1,0:T(8,128)(2,1)S(1)} %bitcast.177, bf16[1,64,128]{2,1,0:T(8,128)(2,1)} %bitcast.175, bf16[1,64,128]{2,1,0:T(8,128)(2,1)S(1)} %bitcast.178), kind=kOutput, calls=%fused_computation.38 | convolution fusion | flops 7795200 | bytes 401664 | tf_op jit(solution)/shard_map/hcuv,ci->uvhi/dot_general | solution.py:56
  26.9 1.1 %fusion.29 = f32[48,136,136,1]{2,1,3,0:T(8,128)S(1)} fusion(f32[3,48,136]{2,0,1:T(4,128)S(1)} %copy.8, f32[3,136]{1,0:T(4,128)S(1)} %get-tuple-element.23, f32[3,48,136]{2,0,1:T(4,128)S(1)} %copy.7, f32[3,136]{1,0:T(4,128)S(1)} %get-tuple-element.24, f32[3,48,136]{2,0,1:T(4,128)S(1)} %copy.6, f32[3,136]{1,0:T(4,128)S(1)} %get-tuple-element.22, ...), kind=kOutput, calls=%fused_computation.49 | convolution fusion | flops 16450560 | bytes 3793584 | tf_op jit(solution)/shard_map/vhai,avj->hij/dot_general | solution.py:75
  28.1 1.1 %fusion.31 = f32[48,136,136,1]{2,1,3,0:T(8,128)S(1)} fusion(f32[3,48,136]{2,0,1:T(4,128)S(1)} %copy.8, f32[3,136]{1,0:T(4,128)S(1)} %get-tuple-element.23, f32[3,48,136]{2,0,1:T(4,128)S(1)} %copy.7, f32[3,136]{1,0:T(4,128)S(1)} %get-tuple-element.24, f32[3,48,136]{2,0,1:T(4,128)S(1)} %copy.6, f32[3,136]{1,0:T(4,128)S(1)} %get-tuple-element.22, ...), kind=kOutput, calls=%fused_computation.50 | convolution fusion | flops 16391808 | bytes 3793584 | tf_op jit(solution)/shard_map/vhai,avj->hij/dot_general | solution.py:74
  29.3 0.3 convolution_bitcast_fusion
  30.2 1.1 %fusion.32 = f32[48,136,136,1]{1,2,3,0:T(8,128)S(1)} fusion(f32[3,48,136]{2,0,1:T(4,128)S(1)} %copy.13, f32[3,136]{1,0:T(4,128)S(1)} %get-tuple-element.26, f32[3,48,136]{2,0,1:T(4,128)S(1)} %copy.12, f32[3,136]{1,0:T(4,128)S(1)} %get-tuple-element.27, f32[3,48,136]{2,0,1:T(4,128)S(1)} %copy.11, f32[3,136]{1,0:T(4,128)S(1)} %get-tuple-element.25, ...), kind=kOutput, calls=%fused_computation.51 | convolution fusion | flops 16391808 | bytes 3793584 | tf_op jit(solution)/shard_map/bui,uhbj->hij/dot_general | solution.py:76
  31.4 2.4 %fusion.4 = bf16[1,48,136,136]{3,2,1,0:T(8,128)(2,1)S(1)} fusion(f32[48,136,136,1]{1,2,3,0:T(8,128)S(1)} %fusion.32, f32[48,136,136,1]{2,1,3,0:T(8,128)S(1)} %fusion.29, f32[48,136,136,1]{2,1,3,0:T(8,128)S(1)} %fusion.31, f32[48]{0:T(128)S(1)} %copy-done.5, pred[136,136]{1,0:T(8,128)(4,1)S(1)} %fusion.58, f32[3,48,136]{2,0,1:T(4,128)S(1)} %copy.13, ...), kind=kOutput, calls=%fused_computation.7 | convolution fusion | flops 22665216 | bytes 12690352 | tf_op jit(solution)/shard_map/bui,uhbj->hij/dot_general | solution.py:77
  33.8 5.6 %slice_bitcast_fusion.7 = (bf16[48,128,128]{2,1,0:T(8,128)(2,1)S(1)}, bf16[48,128,128]{2,1,0:T(8,128)(2,1)S(1)}, bf16[48,128,128]{2,1,0:T(8,128)(2,1)S(1)}, bf16...) fusion(bf16[1,48,136,136]{3,2,1,0:T(8,128)(2,1)S(1)} %fusion.4), kind=kLoop, calls=%fused_computation.17 | loop fusion | bytes 28311552 | tf_op jit(solution)/shard_map/reshape.4
  39.4 1.4 %fusion.19 = f32[128,128,48]{1,2,0:T(8,128)S(1)} fusion(bf16[48,128,128]{2,1,0:T(8,128)(2,1)S(1)} %get-tuple-element.5, bf16[48,48,3,3]{1,0,3,2:T(8,128)(2,1)S(1)} %copy-done.3), kind=kOutput, calls=%fused_computation.32 | convolution fusion | flops 75497472 | bytes 4730880 | tf_op jit(solution)/shard_map/hk,bkij->bhij/dot_general | solution.py:119
  40.8 1.4 %fusion.7 = f32[128,128,48]{1,2,0:T(8,128)S(1)} fusion(bf16[48,128,128]{2,1,0:T(8,128)(2,1)S(1)} %get-tuple-element.7, bf16[48,48,3,3]{1,0,3,2:T(8,128)(2,1)S(1)} %copy-done.3), kind=kOutput, calls=%fused_computation.20 | convolution fusion | flops 75497472 | bytes 4730880 | tf_op jit(solution)/shard_map/hk,bkij->bhij/dot_general | solution.py:119
  42.2 1.4 %fusion.9 = f32[128,128,48]{1,2,0:T(8,128)S(1)} fusion(bf16[48,128,128]{2,1,0:T(8,128)(2,1)S(1)} %get-tuple-element.8, bf16[48,48,3,3]{1,0,3,2:T(8,128)(2,1)S(1)} %copy-done.3), kind=kOutput, calls=%fused_computation.22 | convolution fusion | flops 75497472 | bytes 4730880 | tf_op jit(solution)/shard_map/hk,bkij->bhij/dot_general | solution.py:119
  43.6 1.4 %fusion.11 = f32[128,128,48]{1,2,0:T(8,128)S(1)} fusion(bf16[48,128,128]{2,1,0:T(8,128)(2,1)S(1)} %get-tuple-element.9, bf16[48,48,3,3]{1,0,3,2:T(8,128)(2,1)S(1)} %copy-done.3), kind=kOutput, calls=%fused_computation.24 | convolution fusion | flops 75497472 | bytes 4730880 | tf_op jit(solution)/shard_map/hk,bkij->bhij/dot_general | solution.py:119
  45.0 1.4 %fusion.13 = f32[128,128,48]{1,2,0:T(8,128)S(1)} fusion(bf16[48,128,128]{2,1,0:T(8,128)(2,1)S(1)} %get-tuple-element.10, bf16[48,48,3,3]{1,0,3,2:T(8,128)(2,1)S(1)} %copy-done.3), kind=kOutput, calls=%fused_computation.26 | convolution fusion | flops 75497472 | bytes 4730880 | tf_op jit(solution)/shard_map/hk,bkij->bhij/dot_general | solution.py:119
  46.4 1.4 %fusion.15 = f32[128,128,48]{1,2,0:T(8,128)S(1)} fusion(bf16[48,128,128]{2,1,0:T(8,128)(2,1)S(1)} %get-tuple-element.11, bf16[48,48,3,3]{1,0,3,2:T(8,128)(2,1)S(1)} %copy-done.3), kind=kOutput, calls=%fused_computation.28 | convolution fusion | flops 75497472 | bytes 4730880 | tf_op jit(solution)/shard_map/hk,bkij->bhij/dot_general | solution.py:119
  47.8 1.4 %fusion.17 = f32[128,128,48]{1,2,0:T(8,128)S(1)} fusion(bf16[48,128,128]{2,1,0:T(8,128)(2,1)S(1)} %copy-done.1, bf16[48,48,3,3]{1,0,3,2:T(8,128)(2,1)S(1)} %copy-done.3), kind=kOutput, calls=%fused_computation.30 | convolution fusion | flops 75497472 | bytes 4730880 | tf_op jit(solution)/shard_map/hk,bkij->bhij/dot_general | solution.py:119
  49.2 3.0 %fusion.21 = f32[128,128,48]{1,2,0:T(8,128)} fusion(bf16[48,128,128]{2,1,0:T(8,128)(2,1)S(1)} %copy-done, bf16[48,48,3,3]{1,0,3,2:T(8,128)(2,1)S(1)} %copy-done.3), kind=kOutput, calls=%fused_computation.34 | convolution fusion | flops 75497472 | bytes 4730880 | tf_op jit(solution)/shard_map/hk,bkij->bhij/dot_general | solution.py:119
  52.3 5.8 %fusion.23 = bf16[1,1,1,48,128,128]{5,3,4,2,1,0:T(8,128)(2,1)} fusion(f32[48]{0:T(128)S(1)} %copy-done.6, bf16[48,128,128]{2,1,0:T(8,128)(2,1)S(1)} %get-tuple-element.6, f32[128,128,48]{1,2,0:T(8,128)S(1)} %fusion.7, f32[128,128,48]{1,2,0:T(8,128)S(1)} %fusion.9, f32[128,128,48]{1,2,0:T(8,128)S(1)} %fusion.11, f32[128,128,48]{1,2,0:T(8,128)S(1)} %fusion.13, ...), kind=kOutput, calls=%fused_computation.36 | convolution fusion | flops 83361792 | bytes 28324352 | tf_op jit(solution)/shard_map/hk,bkij->bhij/dot_general | solution.py:119
  58.1 3.0 %copy.27 = bf16[1,1,1,48,128,128]{5,4,3,2,1,0:T(8,128)(2,1)} copy(bf16[1,1,1,48,128,128]{5,3,4,2,1,0:T(8,128)(2,1)} %fusion.23) | data formatting | bytes 3145728 | tf_op jit(solution)/shard_map/broadcast_in_dim | solution.py:126
  (48 shorter events, 1.7 us)
Async XLA Ops:
  0.0 29.3 %collective-permute-start.2 = (bf16[1,1,64,128]{3,2,1,0:T(8,128)(2,1)}, bf16[1,1,64,128]{3,2,1,0:T(8,128)(2,1)S(1)}, u32[]{:S(2)}, u32[]{:S(2)}) collective-permute-start(bf16[1,1,64,128]{3,2,1,0:T(8,128)(2,1)} %param.5), channel_id=1, source_target_pairs={{10,2},{19,3},{28,4},{37,5},{46,6},{55,7},{0,8},{18,10},{27,11},{3... | collective-permute-start | bytes 49160 | tf_op jit(solution)/shard_map/ppermute | solution.py:24
  4.4 20.7 %collective-permute-start.1 = (bf16[1,1,64,128]{3,2,1,0:T(8,128)(2,1)}, bf16[1,1,64,128]{3,2,1,0:T(8,128)(2,1)S(1)}, u32[]{:S(2)}, u32[]{:S(2)}) collective-permute-start(bf16[1,1,64,128]{3,2,1,0:T(8,128)(2,1)} %param.5), channel_id=1, source_target_pairs={{8,0},{9,1},{10,2},{11,3},{12,4},{13,5},{14,6},{15,7},{16,8},{17,9... | collective-permute-start | bytes 49160 | tf_op jit(solution)/shard_map/ppermute | solution.py:24
  7.2 18.0 %collective-permute-start = (bf16[1,1,64,128]{3,2,1,0:T(8,128)(2,1)}, bf16[1,1,64,128]{3,2,1,0:T(8,128)(2,1)S(1)}, u32[]{:S(2)}, u32[]{:S(2)}) collective-permute-start(bf16[1,1,64,128]{3,2,1,0:T(8,128)(2,1)} %param.5), channel_id=1, source_target_pairs={{0,8},{1,9},{2,10},{3,11},{4,12},{5,13},{6,14},{7,15},{8,16},{9,17... | collective-permute-start | bytes 49160 | tf_op jit(solution)/shard_map/ppermute | solution.py:24
  10.3 19.0 %collective-permute-start.4 = (bf16[1,1,64,128]{3,2,1,0:T(8,128)(2,1)}, bf16[1,1,64,128]{3,2,1,0:T(8,128)(2,1)S(1)}, u32[]{:S(2)}, u32[]{:S(2)}) collective-permute-start(bf16[1,1,64,128]{3,2,1,0:T(8,128)(2,1)} %param.5), channel_id=1, source_target_pairs={{8,0},{17,1},{26,2},{35,3},{44,4},{53,5},{62,6},{71,7},{16,8},{25,... | collective-permute-start | bytes 49160 | tf_op jit(solution)/shard_map/ppermute | solution.py:24
  15.0 14.3 %collective-permute-start.3 = (bf16[1,1,64,128]{3,2,1,0:T(8,128)(2,1)}, bf16[1,1,64,128]{3,2,1,0:T(8,128)(2,1)S(1)}, u32[]{:S(2)}, u32[]{:S(2)}) collective-permute-start(bf16[1,1,64,128]{3,2,1,0:T(8,128)(2,1)} %param.5), channel_id=1, source_target_pairs={{9,1},{18,2},{27,3},{36,4},{45,5},{54,6},{63,7},{17,9},{26,10},{35... | collective-permute-start | bytes 49160 | tf_op jit(solution)/shard_map/ppermute | solution.py:24
  28.1 1.2 %copy-start.4 = (bf16[1,1,64,128]{3,2,1,0:T(8,128)(2,1)S(1)}, bf16[1,1,64,128]{3,2,1,0:T(8,128)(2,1)}, u32[]{:S(2)}) copy-start(bf16[1,1,64,128]{3,2,1,0:T(8,128)(2,1)} %param.5) | copy-start | bytes 49156
  28.1 1.2 %copy-start.2 = (bf16[48,128,3,3]{1,0,3,2:T(8,128)(2,1)S(1)}, bf16[48,128,3,3]{1,0,3,2:T(8,128)(2,1)}, u32[]{:S(2)}) copy-start(bf16[48,128,3,3]{1,0,3,2:T(8,128)(2,1)} %param.6) | copy-start | bytes 331780
  30.2 1.2 %copy-start.5 = (f32[48]{0:T(128)S(1)}, f32[48]{0:T(128)}, u32[]{:S(2)}) copy-start(f32[48]{0:T(128)} %param.7) | copy-start | bytes 580
  33.7 5.6 %copy-start.3 = (bf16[48,48,3,3]{1,0,3,2:T(8,128)(2,1)S(1)}, bf16[48,48,3,3]{1,0,3,2:T(8,128)(2,1)}, u32[]{:S(2)}) copy-start(bf16[48,48,3,3]{1,0,3,2:T(8,128)(2,1)} %param.8) | copy-start | bytes 124420
  46.4 1.4 %copy-start.1 = (bf16[48,128,128]{2,1,0:T(8,128)(2,1)S(1)}, bf16[48,128,128]{2,1,0:T(8,128)(2,1)}, u32[]{:S(2)}) copy-start(bf16[48,128,128]{2,1,0:T(8,128)(2,1)} %get-tuple-element.12) | copy-start | bytes 4718596
  47.8 1.4 %copy-start = (bf16[48,128,128]{2,1,0:T(8,128)(2,1)S(1)}, bf16[48,128,128]{2,1,0:T(8,128)(2,1)}, u32[]{:S(2)}) copy-start(bf16[48,128,128]{2,1,0:T(8,128)(2,1)} %get-tuple-element.13) | copy-start | bytes 4718596
  49.2 3.1 %copy-start.6 = (f32[48]{0:T(128)S(1)}, f32[48]{0:T(128)}, u32[]{:S(2)}) copy-start(f32[48]{0:T(128)} %param.9) | copy-start | bytes 580

commit v4 on v3

--- a/solution.py
+++ b/solution.py
@@ -2,6 +2,7 @@
 import jax.numpy as jnp
 from jax import lax
 from jax.sharding import PartitionSpec as P
+from jax.experimental import pallas as pl
 
 
 def band_mask(row_tile, col_tile, start, extent, width, nbins, offsets_total):
@@ -71,11 +72,46 @@
     p_col_hi, p_col_lo = split_bf16(p_col)
     q_col = q_col.astype(jnp.bfloat16)
     q_row = q_row.astype(jnp.bfloat16)
-    term_row = jnp.einsum("vhai,avj->hij", p_row_hi, q_col, preferred_element_type=jnp.float32)
-    term_row = term_row + jnp.einsum("vhai,avj->hij", p_row_lo, q_col, preferred_element_type=jnp.float32)
-    term_col = jnp.einsum("bui,uhbj->hij", q_row, p_col_hi, preferred_element_type=jnp.float32)
-    term_col = term_col + jnp.einsum("bui,uhbj->hij", q_row, p_col_lo, preferred_element_type=jnp.float32)
+    term_row = jnp.einsum("vhai,avj->ihj", p_row_hi, q_col, preferred_element_type=jnp.float32)
+    term_row = term_row + jnp.einsum("vhai,avj->ihj", p_row_lo, q_col, preferred_element_type=jnp.float32)
+    term_col = jnp.einsum("bui,uhbj->ihj", q_row, p_col_hi, preferred_element_type=jnp.float32)
+    term_col = term_col + jnp.einsum("bui,uhbj->ihj", q_row, p_col_lo, preferred_element_type=jnp.float32)
     return term_row + term_col
+
+
+ROWS_PER_STEP = 8
+
+
+def second_conv_kernel(w_ref, b_ref, hidden_ref, out_ref):
+    step = pl.program_id(0)
+    width = out_ref.shape[2]
+    for r in range(ROWS_PER_STEP):
+        i = step * ROWS_PER_STEP + r
+        acc = None
+        for u in range(3):
+            row = hidden_ref[i + 4 * u]
+            for v in range(3):
+                part = jnp.dot(w_ref[3 * u + v], row[:, 4 * v : 4 * v + width],
+                               preferred_element_type=jnp.float32)
+                acc = part if acc is None else acc + part
+        out_ref[:, r, :] = (acc + b_ref[...]).astype(out_ref.dtype)
+
+
+def second_conv(hidden, w_second, b_second):
+    rows_in, hid, cols_in = hidden.shape
+    width = rows_in - 8
+    taps = jnp.transpose(w_second, (2, 3, 0, 1)).reshape(9, hid, hid)
+    return pl.pallas_call(
+        second_conv_kernel,
+        grid=(width // ROWS_PER_STEP,),
+        in_specs=[
+            pl.BlockSpec((9, hid, hid), lambda s: (0, 0, 0)),
+            pl.BlockSpec((hid, 1), lambda s: (0, 0)),
+            pl.BlockSpec((rows_in, hid, cols_in), lambda s: (0, 0, 0)),
+        ],
+        out_specs=pl.BlockSpec((hid, ROWS_PER_STEP, width), lambda s: (0, s, 0)),
+        out_shape=jax.ShapeDtypeStruct((hid, width, width), jnp.bfloat16),
+    )(taps, b_second.reshape(hid, 1), hidden)
 
 
 def local(trunk, w_first, b_first, w_second, b_second):
@@ -104,26 +140,13 @@
     rows = row_line[:, :, width - 6 : width - 6 + extent]
     cols = col_line[:, :, width - 6 : width - 6 + extent]
     pre = first_conv(rows[0], cols[0], w_first, row_tile, col_tile, offset, width, nbins, n_off)
-    pre = pre[None]
     inner_mask = band_mask(row_tile, col_tile, -4, inner_size, width, nbins, n_off)
     hidden = jnp.where(
-        inner_mask[None, None], jnp.maximum(pre + b_first[None, :, None, None], 0.0), 0.0
+        inner_mask[:, None, :], jnp.maximum(pre + b_first[None, :, None], 0.0), 0.0
     )
     hidden = hidden.astype(jnp.bfloat16)
-    result = jnp.zeros((samples, hidden_width, width, width), jnp.float32)
-    for tap_row in range(3):
-        for tap_col in range(3):
-            window_cells = hidden[
-                :, :, 4 * tap_row : 4 * tap_row + width, 4 * tap_col : 4 * tap_col + width
-            ]
-            result = result + jnp.einsum(
-                "hk,bkij->bhij",
-                w_second[:, :, tap_row, tap_col],
-                window_cells,
-                preferred_element_type=jnp.float32,
-            )
-    result = (result + b_second[None, :, None, None]).astype(jnp.bfloat16)
-    return result[None, None]
+    result = second_conv(hidden, w_second, b_second)
+    return result[None, None, None]
 
 
 def solution(mesh):

time: 61.4 us -> 84.4 us (1.37)
  the two profiles are of different devices: /device:TPU:472 before, /device:TPU:452 now
where the time goes in v4:
time: 84.4 us; the launch traced here: 83.9 us
  starting transfers between devices  23.3 us (28%)
  local copies, waits for them, and re-layouts  21.5 us (25%)
  matrix products  15.3 us (18%)
  Pallas kernels  14.5 us (17%)
  other arithmetic  9 us (11%)
    ppermute x5, starting transfers between devices, fetch(): moved = lax.ppermute(trunk, ('diag', 'off'), pairs)  23.3 us
    pallas_call x1, Pallas kernels, second_conv(): pl.pallas_call(second_conv_kernel, grid=(width // ROWS_PER_STEP,), in_spe...  14.5 us
    dot_general x1, local copies, waits for them, and re-layouts, first_conv(): jnp.einsum('vhai,avj->ihj', p_row_lo, q_col, preferred_element_type=jnp.f...  8.63 us
    dot_general x1, local copies, waits for them, and re-layouts, first_conv(): jnp.einsum('vhai,avj->ihj', p_row_hi, q_col, preferred_element_type=jnp.f...  8.6 us
    convert_element_type x1, other arithmetic, local(): hidden = hidden.astype(jnp.bfloat16)  8.06 us
    dot_general x1, matrix products, first_conv(): jnp.einsum('bui,uhbj->ihj', q_row, p_col_lo, preferred_element_type=jnp.f...  4.54 us
    dot_general x1, matrix products, first_conv(): jnp.einsum('vhai,avj->ihj', p_row_lo, q_col, preferred_element_type=jnp.f...  3.96 us
    dot_general x1, matrix products, first_conv(): jnp.einsum('vhai,avj->ihj', p_row_hi, q_col, preferred_element_type=jnp.f...  3.84 us
  transfers between devices with their start and end apart: 5, of which 0 were waited for; matrix products, arithmetic and copies ran while one was open for 35% of the time, Pallas kernels for 0%

profile of v4, /device:TPU:452, one launch (start us, length us, event | category | flops | bytes accessed | tf_op | source)
XLA Modules:
  0.0 83.9 jit_solution(6105861460165711471)
XLA Ops:
  0.0 3.1 %collective-permute-start = (bf16[1,1,64,128]{3,2,1,0:T(8,128)(2,1)}, bf16[1,1,64,128]{3,2,1,0:T(8,128)(2,1)S(1)}, u32[]{:S(2)}, u32[]{:S(2)}) collective-permute-start(bf16[1,1,64,128]{3,2,1,0:T(8,128)(2,1)} %param.5), channel_id=1, source_target_pairs={{0,8},{1,9},{2,10},{3,11},{4,12},{5,13},{6,14},{7,15},{8,16},{9,17... | collective-permute-start | bytes 49160 | tf_op jit(solution)/shard_map/ppermute | solution.py:25
  3.1 2.7 %collective-permute-start.1 = (bf16[1,1,64,128]{3,2,1,0:T(8,128)(2,1)}, bf16[1,1,64,128]{3,2,1,0:T(8,128)(2,1)S(1)}, u32[]{:S(2)}, u32[]{:S(2)}) collective-permute-start(bf16[1,1,64,128]{3,2,1,0:T(8,128)(2,1)} %param.5), channel_id=1, source_target_pairs={{8,0},{9,1},{10,2},{11,3},{12,4},{13,5},{14,6},{15,7},{16,8},{17,9... | collective-permute-start | bytes 49160 | tf_op jit(solution)/shard_map/ppermute | solution.py:25
  5.9 5.3 %collective-permute-start.2 = (bf16[1,1,64,128]{3,2,1,0:T(8,128)(2,1)}, bf16[1,1,64,128]{3,2,1,0:T(8,128)(2,1)S(1)}, u32[]{:S(2)}, u32[]{:S(2)}) collective-permute-start(bf16[1,1,64,128]{3,2,1,0:T(8,128)(2,1)} %param.5), channel_id=1, source_target_pairs={{10,2},{19,3},{28,4},{37,5},{46,6},{55,7},{0,8},{18,10},{27,11},{3... | collective-permute-start | bytes 49160 | tf_op jit(solution)/shard_map/ppermute | solution.py:25
  11.2 6.2 %collective-permute-start.3 = (bf16[1,1,64,128]{3,2,1,0:T(8,128)(2,1)}, bf16[1,1,64,128]{3,2,1,0:T(8,128)(2,1)S(1)}, u32[]{:S(2)}, u32[]{:S(2)}) collective-permute-start(bf16[1,1,64,128]{3,2,1,0:T(8,128)(2,1)} %param.5), channel_id=1, source_target_pairs={{9,1},{18,2},{27,3},{36,4},{45,5},{54,6},{63,7},{17,9},{26,10},{35... | collective-permute-start | bytes 49160 | tf_op jit(solution)/shard_map/ppermute | solution.py:25
  17.4 5.9 %collective-permute-start.4 = (bf16[1,1,64,128]{3,2,1,0:T(8,128)(2,1)}, bf16[1,1,64,128]{3,2,1,0:T(8,128)(2,1)S(1)}, u32[]{:S(2)}, u32[]{:S(2)}) collective-permute-start(bf16[1,1,64,128]{3,2,1,0:T(8,128)(2,1)} %param.5), channel_id=1, source_target_pairs={{8,0},{17,1},{26,2},{35,3},{44,4},{53,5},{62,6},{71,7},{16,8},{25,... | collective-permute-start | bytes 49160 | tf_op jit(solution)/shard_map/ppermute | solution.py:25
  23.4 0.1 convolution_convert_fusion.1
  23.6 0.2 convolution_convert_fusion
  24.0 0.1 fusion.11
  24.2 1.3 %copy.20.b_ref = f32[48,1]{1,0:T(8,128)} copy(f32[48,1]{0,1:T(1,128)} %bitcast.98) | data formatting | bytes 384 | tf_op jit(solution)/shard_map/reshape | solution.py:114
  25.5 1.2 %convolution_bitcast_fusion.5 = f32[3,3,48,140]{3,2,1,0:T(8,128)S(1)} fusion(bf16[48,128,3,3]{1,0,3,2:T(8,128)(2,1)} %param.6, bf16[1,64,128]{2,1,0:T(8,128)(2,1)S(1)} %bitcast.97, bf16[1,64,128]{2,1,0:T(8,128)(2,1)} %bitcast.94, bf16[1,64,128]{2,1,0:T(8,128)(2,1)S(1)} %bitcast.96), kind=kOutput, calls=%fused_computation.11 | convolution fusion | flops 7795200 | bytes 401664 | tf_op jit(solution)/shard_map/hcuv,ci->uvhi/dot_general | solution.py:57
  26.9 0.1 copy.7
  27.1 0.1 copy.8
  27.3 0.4 fusion.4
  27.7 3.8 %convolution_bitcast_fusion.3 = f32[136,48,136]{2,0,1:T(8,128)} fusion(bf16[3,48,3,136]{3,0,2,1:T(4,128)(2,1)S(1)} %get-tuple-element.6, bf16[3,1,136]{2,0,1:T(4,128)(2,1)S(1)} %get-tuple-element.24, bf16[3,1,136]{2,0,1:T(4,128)(2,1)S(1)} %get-tuple-element.25, bf16[3,1,136]{2,0,1:T(4,128)(2,1)S(1)} %get-tuple-element.23), kind=kOutput, calls=%fused_computation.9 | convolution fusion | flops 15987888 | bytes 3671184 | tf_op jit(solution)/shard_map/vhai,avj->ihj/dot_general | solution.py:75
  31.5 4.0 %convolution_bitcast_fusion.2 = f32[136,48,136]{2,0,1:T(8,128)} fusion(bf16[3,48,3,136]{3,0,2,1:T(4,128)(2,1)S(1)} %get-tuple-element.5, bf16[3,1,136]{2,0,1:T(4,128)(2,1)S(1)} %get-tuple-element.24, bf16[3,1,136]{2,0,1:T(4,128)(2,1)S(1)} %get-tuple-element.25, bf16[3,1,136]{2,0,1:T(4,128)(2,1)S(1)} %get-tuple-element.23), kind=kOutput, calls=%fused_computation.8 | convolution fusion | flops 15987888 | bytes 3671184 | tf_op jit(solution)/shard_map/vhai,avj->ihj/dot_general | solution.py:76
  35.5 8.6 %copy.11 = f32[136,48,136]{0,1,2:T(8,128)} copy(f32[136,48,136]{2,0,1:T(8,128)} %convolution_bitcast_fusion.3) | data formatting | bytes 7102464 | tf_op jit(solution)/shard_map/vhai,avj->ihj/dot_general | solution.py:75
  44.1 8.6 %copy.12 = f32[136,48,136]{0,1,2:T(8,128)} copy(f32[136,48,136]{2,0,1:T(8,128)} %convolution_bitcast_fusion.2) | data formatting | bytes 7102464 | tf_op jit(solution)/shard_map/vhai,avj->ihj/dot_general | solution.py:76
  52.8 0.3 convolution_bitcast_fusion.4
  53.6 0.4 reduce-precision_convert_fusion
  54.0 1.1 %convolution_bitcast_fusion.1 = f32[136,48,136]{2,0,1:T(8,128)S(1)} fusion(bf16[3,48,3,136]{3,0,2,1:T(4,128)(2,1)S(1)} %get-tuple-element.7, bf16[3,1,136]{2,0,1:T(4,128)(2,1)S(1)} %get-tuple-element.27, bf16[3,1,136]{2,0,1:T(4,128)(2,1)S(1)} %get-tuple-element.28, bf16[3,1,136]{2,0,1:T(4,128)(2,1)S(1)} %get-tuple-element.26), kind=kOutput, calls=%fused_computation.7 | convolution fusion | flops 15987888 | bytes 3671184 | tf_op jit(solution)/shard_map/bui,uhbj->ihj/dot_general | solution.py:77
  55.2 4.5 %convolution_bitcast_fusion = f32[136,48,136]{2,0,1:T(8,128)} fusion(bf16[3,48,3,136]{3,0,2,1:T(4,128)(2,1)S(1)} %get-tuple-element.8, bf16[3,1,136]{2,0,1:T(4,128)(2,1)S(1)} %get-tuple-element.27, bf16[3,1,136]{2,0,1:T(4,128)(2,1)S(1)} %get-tuple-element.28, bf16[3,1,136]{2,0,1:T(4,128)(2,1)S(1)} %get-tuple-element.26), kind=kOutput, calls=%fused_computation.6 | convolution fusion | flops 15987888 | bytes 3671184 | tf_op jit(solution)/shard_map/bui,uhbj->ihj/dot_general | solution.py:78
  59.7 1.6 %copy-done = f32[136,48,136]{0,1,2:T(8,128)S(1)} copy-done((f32[136,48,136]{0,1,2:T(8,128)S(1)}, f32[136,48,136]{0,1,2:T(8,128)}, u32[]{:S(2)}) %copy-start) | copy-done | bytes 3551256
  61.3 8.1 %fusion.3.hidden_ref = bf16[136,48,136]{2,1,0:T(8,128)(2,1)} fusion(f32[136,48,136]{2,0,1:T(8,128)} %convolution_bitcast_fusion, f32[136,48,136]{2,0,1:T(8,128)S(1)} %convolution_bitcast_fusion.1, f32[136,48,136]{0,1,2:T(8,128)S(1)} %bitcast.90, f32[136,48,136]{0,1,2:T(8,128)S(1)} %copy-done, f32[48]{0:T(128)S(1)} %copy-done.3, pred[136,136]{1,0:T(8,128)(4,1)S(1)} %fusion.11), kind=kLoop, calls=%fused_computation.4 | loop fusion | flops 6214656 | bytes 15999232 | tf_op jit(solution)/shard_map/convert_element_type | solution.py:147
  69.4 14.5 %shard_map.55 = bf16[48,128,128]{2,1,0:T(8,128)(2,1)} custom-call(bf16[9,48,48]{2,1,0:T(8,128)(2,1)} %bitcast.93, f32[48,1]{1,0:T(8,128)} %copy.20.b_ref, bf16[136,48,136]{2,1,0:T(8,128)(2,1)} %fusion.3.hidden_ref), custom_call_target="tpu_custom_call" | custom-call | tf_op jit(solution)/shard_map/pallas_call | solution.py:104
  (41 shorter events, 1.3 us)
Async XLA Ops:
  0.0 25.5 %collective-permute-start = (bf16[1,1,64,128]{3,2,1,0:T(8,128)(2,1)}, bf16[1,1,64,128]{3,2,1,0:T(8,128)(2,1)S(1)}, u32[]{:S(2)}, u32[]{:S(2)}) collective-permute-start(bf16[1,1,64,128]{3,2,1,0:T(8,128)(2,1)} %param.5), channel_id=1, source_target_pairs={{0,8},{1,9},{2,10},{3,11},{4,12},{5,13},{6,14},{7,15},{8,16},{9,17... | collective-permute-start | bytes 49160 | tf_op jit(solution)/shard_map/ppermute | solution.py:25
  3.1 22.4 %collective-permute-start.1 = (bf16[1,1,64,128]{3,2,1,0:T(8,128)(2,1)}, bf16[1,1,64,128]{3,2,1,0:T(8,128)(2,1)S(1)}, u32[]{:S(2)}, u32[]{:S(2)}) collective-permute-start(bf16[1,1,64,128]{3,2,1,0:T(8,128)(2,1)} %param.5), channel_id=1, source_target_pairs={{8,0},{9,1},{10,2},{11,3},{12,4},{13,5},{14,6},{15,7},{16,8},{17,9... | collective-permute-start | bytes 49160 | tf_op jit(solution)/shard_map/ppermute | solution.py:25
  5.9 29.7 %collective-permute-start.2 = (bf16[1,1,64,128]{3,2,1,0:T(8,128)(2,1)}, bf16[1,1,64,128]{3,2,1,0:T(8,128)(2,1)S(1)}, u32[]{:S(2)}, u32[]{:S(2)}) collective-permute-start(bf16[1,1,64,128]{3,2,1,0:T(8,128)(2,1)} %param.5), channel_id=1, source_target_pairs={{10,2},{19,3},{28,4},{37,5},{46,6},{55,7},{0,8},{18,10},{27,11},{3... | collective-permute-start | bytes 49160 | tf_op jit(solution)/shard_map/ppermute | solution.py:25
  11.2 24.3 %collective-permute-start.3 = (bf16[1,1,64,128]{3,2,1,0:T(8,128)(2,1)}, bf16[1,1,64,128]{3,2,1,0:T(8,128)(2,1)S(1)}, u32[]{:S(2)}, u32[]{:S(2)}) collective-permute-start(bf16[1,1,64,128]{3,2,1,0:T(8,128)(2,1)} %param.5), channel_id=1, source_target_pairs={{9,1},{18,2},{27,3},{36,4},{45,5},{54,6},{63,7},{17,9},{26,10},{35... | collective-permute-start | bytes 49160 | tf_op jit(solution)/shard_map/ppermute | solution.py:25
  17.4 35.3 %collective-permute-start.4 = (bf16[1,1,64,128]{3,2,1,0:T(8,128)(2,1)}, bf16[1,1,64,128]{3,2,1,0:T(8,128)(2,1)S(1)}, u32[]{:S(2)}, u32[]{:S(2)}) collective-permute-start(bf16[1,1,64,128]{3,2,1,0:T(8,128)(2,1)} %param.5), channel_id=1, source_target_pairs={{8,0},{17,1},{26,2},{35,3},{44,4},{53,5},{62,6},{71,7},{16,8},{25,... | collective-permute-start | bytes 49160 | tf_op jit(solution)/shard_map/ppermute | solution.py:25
  27.7 7.8 %copy-start.2 = (bf16[1,1,64,128]{3,2,1,0:T(8,128)(2,1)S(1)}, bf16[1,1,64,128]{3,2,1,0:T(8,128)(2,1)}, u32[]{:S(2)}) copy-start(bf16[1,1,64,128]{3,2,1,0:T(8,128)(2,1)} %param.5) | copy-start | bytes 49156
  44.1 8.6 %copy-start.1 = (bf16[48,128,3,3]{1,0,3,2:T(8,128)(2,1)S(1)}, bf16[48,128,3,3]{1,0,3,2:T(8,128)(2,1)}, u32[]{:S(2)}) copy-start(bf16[48,128,3,3]{1,0,3,2:T(8,128)(2,1)} %param.6) | copy-start | bytes 331780
  54.0 5.7 %slice-start = ((s8[6684672]{0:T(1024)(128)(4,1)}), s8[4194304]{0:T(1024)(128)(4,1)S(1)}, s32[]{:S(2)}) async-start(s8[6684672]{0:T(1024)(128)(4,1)} %bitcast.89), calls=%async_computation | async-start | bytes 8388608
  54.0 5.7 %slice-start.1 = ((s8[6684672]{0:T(1024)(128)(4,1)}), s8[2490368]{0:T(1024)(128)(4,1)S(1)}, s32[]{:S(2)}) async-start(s8[6684672]{0:T(1024)(128)(4,1)} %bitcast.89), calls=%async_computation.1 | async-start | bytes 4980736
  54.0 7.3 %copy-start = (f32[136,48,136]{0,1,2:T(8,128)S(1)}, f32[136,48,136]{0,1,2:T(8,128)}, u32[]{:S(2)}) copy-start(f32[136,48,136]{0,1,2:T(8,128)} %copy.12) | copy-start | bytes 10653700
  54.0 7.3 %copy-start.3 = (f32[48]{0:T(128)S(1)}, f32[48]{0:T(128)}, u32[]{:S(2)}) copy-start(f32[48]{0:T(128)} %param.7) | copy-start | bytes 580

commit v5 on v4

--- a/solution.py
+++ b/solution.py
@@ -68,14 +68,20 @@
     )
     a_sel = jnp.einsum("ab,ai->bi", g, a_ind)
     q_row = jnp.stack([a_sel[:, 2 * u : 2 * u + size] for u in range(3)], axis=1)
+    taps = 9
+    hid = p_row.shape[1]
+    p_row = jnp.transpose(p_row, (3, 1, 2, 0)).reshape(size, hid, taps)
+    p_col = jnp.transpose(p_col, (2, 0, 1, 3)).reshape(taps, hid, size)
     p_row_hi, p_row_lo = split_bf16(p_row)
     p_col_hi, p_col_lo = split_bf16(p_col)
-    q_col = q_col.astype(jnp.bfloat16)
-    q_row = q_row.astype(jnp.bfloat16)
-    term_row = jnp.einsum("vhai,avj->ihj", p_row_hi, q_col, preferred_element_type=jnp.float32)
-    term_row = term_row + jnp.einsum("vhai,avj->ihj", p_row_lo, q_col, preferred_element_type=jnp.float32)
-    term_col = jnp.einsum("bui,uhbj->ihj", q_row, p_col_hi, preferred_element_type=jnp.float32)
-    term_col = term_col + jnp.einsum("bui,uhbj->ihj", q_row, p_col_lo, preferred_element_type=jnp.float32)
+    q_col = q_col.reshape(taps, size).astype(jnp.bfloat16)
+    q_row = jnp.transpose(q_row, (2, 0, 1)).reshape(size, taps).astype(jnp.bfloat16)
+    p_row_both = jnp.concatenate([p_row_hi, p_row_lo], axis=2)
+    p_col_both = jnp.concatenate([p_col_hi, p_col_lo], axis=0)
+    term_row = jnp.einsum("ihk,kj->ihj", p_row_both, jnp.concatenate([q_col, q_col], axis=0),
+                          preferred_element_type=jnp.float32)
+    term_col = jnp.einsum("ik,khj->ihj", jnp.concatenate([q_row, q_row], axis=1), p_col_both,
+                          preferred_element_type=jnp.float32)
     return term_row + term_col
 
 
@@ -144,8 +150,7 @@
     hidden = jnp.where(
         inner_mask[:, None, :], jnp.maximum(pre + b_first[None, :, None], 0.0), 0.0
     )
-    hidden = hidden.astype(jnp.bfloat16)
-    result = second_conv(hidden, w_second, b_second)
+    result = second_conv(hidden.astype(jnp.bfloat16), w_second, b_second)
     return result[None, None, None]
 
 

time: 84.4 us -> 51.4 us (0.61)
  local copies, waits for them, and re-layouts: 21.5 us -> 2.64 us
  other arithmetic: 9 us -> 1.38 us
  matrix products: 15.3 us -> 8.85 us
    dot_general x2 -> x0, local copies, waits for them, and re-layouts: 17.2 us -> none  [the longest x1 8.63 us: first_conv(): jnp.einsum('vhai,avj->ihj', p_row_lo, q_col, preferred_element_type=jnp.f...]
    convert_element_type x1, other arithmetic: 8.06 us -> 0.01 us  [first_conv(): jnp.transpose(q_row, (2, 0, 1)).reshape(size, taps).astype(jnp.bfloat16)]
    dot_general x4 -> x2, matrix products: 13.5 us -> 6.18 us  [the longest x1 5.12 us: first_conv(): jnp.einsum('ihk,kj->ihj', p_row_both, jnp.concatenate([q_col, q_col], axi...]
    unnamed x12 -> x2, local copies, waits for them, and re-layouts: 1.59 us -> 0.01 us
    dot_general x1, matrix products: 0.27 us -> 1.17 us  [first_conv(): jnp.einsum('hcuv,cj->uvhj', w_first[:, channels:], cols, preferred_elemen...]
  transfers between devices with their start and end apart: 5 -> 5, of which waited for: 0 -> 0; matrix products, arithmetic and copies ran while one was open for 35% -> 10% of each run, Pallas kernels for 0% -> 0%
where the time goes in v5:
time: 51.4 us; the launch traced here: 51 us
  starting transfers between devices  23.3 us (45%)
  Pallas kernels  14.5 us (28%)
  matrix products  8.85 us (17%)
  local copies, waits for them, and re-layouts  2.64 us (5%)
  other arithmetic  1.38 us (3%)
    ppermute x5, starting transfers between devices, fetch(): moved = lax.ppermute(trunk, ('diag', 'off'), pairs)  23.3 us
    pallas_call x1, Pallas kernels, second_conv(): pl.pallas_call(second_conv_kernel, grid=(width // ROWS_PER_STEP,), in_spe...  14.5 us
    dot_general x1, matrix products, first_conv(): jnp.einsum('ihk,kj->ihj', p_row_both, jnp.concatenate([q_col, q_col], axi...  5.12 us
    reshape x1, local copies, waits for them, and re-layouts, second_conv(): b_second.reshape(hid, 1)  1.34 us
    dot_general x1, matrix products, first_conv(): jnp.einsum('hcuv,ci->uvhi', w_first[:, :channels], rows, preferred_elemen...  1.19 us
    dot_general x1, matrix products, first_conv(): jnp.einsum('hcuv,cj->uvhj', w_first[:, channels:], cols, preferred_elemen...  1.17 us
    dot_general x1, matrix products, first_conv(): jnp.einsum('ik,khj->ihj', jnp.concatenate([q_row, q_row], axis=1), p_col_...  1.06 us
  transfers between devices with their start and end apart: 5, of which 0 were waited for; matrix products, arithmetic and copies ran while one was open for 10% of the time, Pallas kernels for 0%

profile of v5, /device:TPU:452, one launch (start us, length us, event | category | flops | bytes accessed | tf_op | source)
XLA Modules:
  0.0 51.0 jit_solution(11276628028994326681)
XLA Ops:
  0.0 3.1 %collective-permute-start = (bf16[1,1,64,128]{3,2,1,0:T(8,128)(2,1)}, bf16[1,1,64,128]{3,2,1,0:T(8,128)(2,1)S(1)}, u32[]{:S(2)}, u32[]{:S(2)}) collective-permute-start(bf16[1,1,64,128]{3,2,1,0:T(8,128)(2,1)} %param.5), channel_id=1, source_target_pairs={{0,8},{1,9},{2,10},{3,11},{4,12},{5,13},{6,14},{7,15},{8,16},{9,17... | collective-permute-start | bytes 49160 | tf_op jit(solution)/shard_map/ppermute | solution.py:25
  3.1 2.7 %collective-permute-start.1 = (bf16[1,1,64,128]{3,2,1,0:T(8,128)(2,1)}, bf16[1,1,64,128]{3,2,1,0:T(8,128)(2,1)S(1)}, u32[]{:S(2)}, u32[]{:S(2)}) collective-permute-start(bf16[1,1,64,128]{3,2,1,0:T(8,128)(2,1)} %param.5), channel_id=1, source_target_pairs={{8,0},{9,1},{10,2},{11,3},{12,4},{13,5},{14,6},{15,7},{16,8},{17,9... | collective-permute-start | bytes 49160 | tf_op jit(solution)/shard_map/ppermute | solution.py:25
  5.9 5.3 %collective-permute-start.2 = (bf16[1,1,64,128]{3,2,1,0:T(8,128)(2,1)}, bf16[1,1,64,128]{3,2,1,0:T(8,128)(2,1)S(1)}, u32[]{:S(2)}, u32[]{:S(2)}) collective-permute-start(bf16[1,1,64,128]{3,2,1,0:T(8,128)(2,1)} %param.5), channel_id=1, source_target_pairs={{10,2},{19,3},{28,4},{37,5},{46,6},{55,7},{0,8},{18,10},{27,11},{3... | collective-permute-start | bytes 49160 | tf_op jit(solution)/shard_map/ppermute | solution.py:25
  11.2 6.2 %collective-permute-start.3 = (bf16[1,1,64,128]{3,2,1,0:T(8,128)(2,1)}, bf16[1,1,64,128]{3,2,1,0:T(8,128)(2,1)S(1)}, u32[]{:S(2)}, u32[]{:S(2)}) collective-permute-start(bf16[1,1,64,128]{3,2,1,0:T(8,128)(2,1)} %param.5), channel_id=1, source_target_pairs={{9,1},{18,2},{27,3},{36,4},{45,5},{54,6},{63,7},{17,9},{26,10},{35... | collective-permute-start | bytes 49160 | tf_op jit(solution)/shard_map/ppermute | solution.py:25
  17.4 5.9 %collective-permute-start.4 = (bf16[1,1,64,128]{3,2,1,0:T(8,128)(2,1)}, bf16[1,1,64,128]{3,2,1,0:T(8,128)(2,1)S(1)}, u32[]{:S(2)}, u32[]{:S(2)}) collective-permute-start(bf16[1,1,64,128]{3,2,1,0:T(8,128)(2,1)} %param.5), channel_id=1, source_target_pairs={{8,0},{17,1},{26,2},{35,3},{44,4},{53,5},{62,6},{71,7},{16,8},{25,... | collective-permute-start | bytes 49160 | tf_op jit(solution)/shard_map/ppermute | solution.py:25
  23.4 0.2 convolution_convert_fusion
  23.6 0.1 convolution_convert_fusion.1
  23.9 0.1 slice_bitcast_fusion.14
  24.1 0.1 fusion.13
  24.5 1.3 %copy.32.b_ref = f32[48,1]{1,0:T(8,128)} copy(f32[48,1]{0,1:T(1,128)} %bitcast.143) | data formatting | bytes 384 | tf_op jit(solution)/shard_map/reshape | solution.py:120
  25.8 1.2 %convolution_bitcast_fusion.1 = f32[3,3,48,140]{3,2,1,0:T(8,128)S(1)} fusion(bf16[48,128,3,3]{1,0,3,2:T(8,128)(2,1)} %param.6, bf16[1,64,128]{2,1,0:T(8,128)(2,1)S(1)} %bitcast.142, bf16[1,64,128]{2,1,0:T(8,128)(2,1)} %bitcast.139, bf16[1,64,128]{2,1,0:T(8,128)(2,1)S(1)} %bitcast.141), kind=kOutput, calls=%fused_computation.6 | convolution fusion | flops 7795200 | bytes 401664 | tf_op jit(solution)/shard_map/hcuv,ci->uvhi/dot_general | solution.py:57
  27.0 0.1 slice_bitcast_fusion.3
  27.2 0.1 reduce-precision_convert_fusion.1
  27.4 0.7 %select_bitcast_fusion.1 = (bf16[1,64,128]{2,1,0:T(8,128)(2,1)S(1)}, bf16[1,64,128]{2,1,0:T(8,128)(2,1)S(1)}) fusion(bf16[1,1,64,128]{3,2,1,0:T(8,128)(2,1)} %param.5, bf16[1,1,64,128]{3,2,1,0:T(8,128)(2,1)S(1)} %collective-permute-done.2, pred[]{:T(512)S(6)} %eq.38, bf16[1,1,64,128]{3,2,1,0:T(8,128)(2,1)S(1)} %collective-permute-done.3, pred[]{:T(512)S(6)} %eq.39), kind=kLoop, calls=%fused_computation.53 | loop fusion | flops 16384 | bytes 81922 | tf_op jit(solution)/shard_map/squeeze | solution.py:142
  28.1 0.1 pad_maximum_fusion
  28.2 0.5 copy.28
  28.7 1.2 %convolution_bitcast_fusion = f32[3,3,48,140]{3,2,1,0:T(8,128)S(1)} fusion(bf16[48,128,3,3]{1,0,3,2:T(8,128)(2,1)} %param.6, bf16[1,64,128]{2,1,0:T(8,128)(2,1)S(1)} %bitcast.140, bf16[1,64,128]{2,1,0:T(8,128)(2,1)S(1)} %get-tuple-element.16, bf16[1,64,128]{2,1,0:T(8,128)(2,1)S(1)} %get-tuple-element.15), kind=kOutput, calls=%fused_computation.5 | convolution fusion | flops 7795200 | bytes 401664 | tf_op jit(solution)/shard_map/hcuv,cj->uvhj/dot_general | solution.py:58
  29.9 0.1 slice.138
  30.0 0.1 slice.141
  30.1 0.1 reduce-precision_convert_fusion
  30.2 0.1 pad_maximum_fusion.1
  30.3 1.1 %fusion.4 = f32[136,48,136]{2,0,1:T(8,128)S(1)} fusion(bf16[18,48,136]{2,1,0:T(8,128)(2,1)S(1)} %pad_maximum_fusion.1, bf16[136,9]{0,1:T(8,128)(2,1)S(1)} %convert_element_type.38), kind=kOutput, calls=%fused_computation.13 | convolution fusion | flops 31970880 | bytes 3788688 | tf_op jit(solution)/shard_map/ik,khj->ihj/dot_general | solution.py:83
  31.4 5.1 %fusion.3.hidden_ref = bf16[136,48,136]{2,1,0:T(8,128)(2,1)} fusion(f32[136,48,136]{2,0,1:T(8,128)S(1)} %fusion.4, f32[48]{0:T(128)S(1)} %copy-done, pred[136,136]{1,0:T(8,128)(4,1)S(1)} %fusion.13, bf16[136,48,18]{1,2,0:T(8,128)(2,1)S(1)} %copy.28, bf16[9,136]{1,0:T(8,128)(2,1)S(1)} %convert_element_type.36), kind=kOutput, calls=%fused_computation.4 | convolution fusion | flops 36409920 | bytes 5582992 | tf_op jit(solution)/shard_map/ihk,kj->ihj/dot_general | solution.py:81
  36.5 14.5 %shard_map.55 = bf16[48,128,128]{2,1,0:T(8,128)(2,1)} custom-call(bf16[9,48,48]{2,1,0:T(8,128)(2,1)} %bitcast.138, f32[48,1]{1,0:T(8,128)} %copy.32.b_ref, bf16[136,48,136]{2,1,0:T(8,128)(2,1)} %fusion.3.hidden_ref), custom_call_target="tpu_custom_call" | custom-call | tf_op jit(solution)/shard_map/pallas_call | solution.py:110
  (40 shorter events, 0.6 us)
Async XLA Ops:
  0.0 25.8 %collective-permute-start = (bf16[1,1,64,128]{3,2,1,0:T(8,128)(2,1)}, bf16[1,1,64,128]{3,2,1,0:T(8,128)(2,1)S(1)}, u32[]{:S(2)}, u32[]{:S(2)}) collective-permute-start(bf16[1,1,64,128]{3,2,1,0:T(8,128)(2,1)} %param.5), channel_id=1, source_target_pairs={{0,8},{1,9},{2,10},{3,11},{4,12},{5,13},{6,14},{7,15},{8,16},{9,17... | collective-permute-start | bytes 49160 | tf_op jit(solution)/shard_map/ppermute | solution.py:25
  3.1 22.7 %collective-permute-start.1 = (bf16[1,1,64,128]{3,2,1,0:T(8,128)(2,1)}, bf16[1,1,64,128]{3,2,1,0:T(8,128)(2,1)S(1)}, u32[]{:S(2)}, u32[]{:S(2)}) collective-permute-start(bf16[1,1,64,128]{3,2,1,0:T(8,128)(2,1)} %param.5), channel_id=1, source_target_pairs={{8,0},{9,1},{10,2},{11,3},{12,4},{13,5},{14,6},{15,7},{16,8},{17,9... | collective-permute-start | bytes 49160 | tf_op jit(solution)/shard_map/ppermute | solution.py:25
  5.9 21.5 %collective-permute-start.2 = (bf16[1,1,64,128]{3,2,1,0:T(8,128)(2,1)}, bf16[1,1,64,128]{3,2,1,0:T(8,128)(2,1)S(1)}, u32[]{:S(2)}, u32[]{:S(2)}) collective-permute-start(bf16[1,1,64,128]{3,2,1,0:T(8,128)(2,1)} %param.5), channel_id=1, source_target_pairs={{10,2},{19,3},{28,4},{37,5},{46,6},{55,7},{0,8},{18,10},{27,11},{3... | collective-permute-start | bytes 49160 | tf_op jit(solution)/shard_map/ppermute | solution.py:25
  11.2 16.2 %collective-permute-start.3 = (bf16[1,1,64,128]{3,2,1,0:T(8,128)(2,1)}, bf16[1,1,64,128]{3,2,1,0:T(8,128)(2,1)S(1)}, u32[]{:S(2)}, u32[]{:S(2)}) collective-permute-start(bf16[1,1,64,128]{3,2,1,0:T(8,128)(2,1)} %param.5), channel_id=1, source_target_pairs={{9,1},{18,2},{27,3},{36,4},{45,5},{54,6},{63,7},{17,9},{26,10},{35... | collective-permute-start | bytes 49160 | tf_op jit(solution)/shard_map/ppermute | solution.py:25
  17.4 11.2 %collective-permute-start.4 = (bf16[1,1,64,128]{3,2,1,0:T(8,128)(2,1)}, bf16[1,1,64,128]{3,2,1,0:T(8,128)(2,1)S(1)}, u32[]{:S(2)}, u32[]{:S(2)}) collective-permute-start(bf16[1,1,64,128]{3,2,1,0:T(8,128)(2,1)} %param.5), channel_id=1, source_target_pairs={{8,0},{17,1},{26,2},{35,3},{44,4},{53,5},{62,6},{71,7},{16,8},{25,... | collective-permute-start | bytes 49160 | tf_op jit(solution)/shard_map/ppermute | solution.py:25
  28.1 3.3 %copy-start = (f32[48]{0:T(128)S(1)}, f32[48]{0:T(128)}, u32[]{:S(2)}) copy-start(f32[48]{0:T(128)} %param.7) | copy-start | bytes 580

commit v6 on v5

--- a/solution.py
+++ b/solution.py
@@ -134,12 +134,19 @@
 
     row_prev = fetch(trunk, lambda o: -1, n_diag, n_off, offset)
     row_next = fetch(trunk, lambda o: 1, n_diag, n_off, offset)
-    col_prev = fetch(trunk, lambda o: o - 1, n_diag, n_off, offset)
-    col_here = fetch(trunk, lambda o: o, n_diag, n_off, offset)
-    col_next = fetch(trunk, lambda o: o + 1, n_diag, n_off, offset)
+    row_after = fetch(trunk, lambda o: 2, n_diag, n_off, offset)
+    line = jnp.concatenate([row_prev, trunk, row_next, row_after], axis=0)
+    pairs = [
+        ((d + o - 1) * n_off + o, d * n_off + o)
+        for d in range(n_diag)
+        for o in range(2, n_off)
+        if d + o - 1 < n_diag
+    ]
+    moved = lax.ppermute(line, ("diag", "off"), pairs)
+    col_panels = jnp.where(offset == 0, line[0:3], jnp.where(offset == 1, line[1:4], moved[1:4]))
 
-    row_line = jnp.concatenate([row_prev[0], trunk[0], row_next[0]], axis=-1)
-    col_line = jnp.concatenate([col_prev[0], col_here[0], col_next[0]], axis=-1)
+    row_line = jnp.concatenate([line[0], line[1], line[2]], axis=-1)
+    col_line = jnp.concatenate([col_panels[0], col_panels[1], col_panels[2]], axis=-1)
 
     extent = width + 12
     inner_size = width + 8

time: 51.4 us -> 51.9 us (level)
  the two profiles are of different devices: /device:TPU:452 before, /device:TPU:446 now
where the time goes in v6:
time: 51.9 us; the launch traced here: 51.4 us
  Pallas kernels  14.5 us (28%)
  waiting for transfers between devices  11.8 us (23%)
  starting transfers between devices  11.1 us (21%)
  matrix products  8.85 us (17%)
  local copies, waits for them, and re-layouts  2.65 us (5%)
  other arithmetic  2.19 us (4%)
    pallas_call x1, Pallas kernels, second_conv(): pl.pallas_call(second_conv_kernel, grid=(width // ROWS_PER_STEP,), in_spe...  14.5 us
    ppermute x3, starting transfers between devices, fetch(): moved = lax.ppermute(trunk, ('diag', 'off'), pairs)  9.15 us
    ppermute x1, waiting for transfers between devices, local(): moved = lax.ppermute(line, ('diag', 'off'), pairs)  8.5 us
    dot_general x1, matrix products, first_conv(): jnp.einsum('ihk,kj->ihj', p_row_both, jnp.concatenate([q_col, q_col], axi...  5.12 us
    ppermute x3, waiting for transfers between devices, fetch(): moved = lax.ppermute(trunk, ('diag', 'off'), pairs)  3.29 us
    ppermute x1, starting transfers between devices, local(): moved = lax.ppermute(line, ('diag', 'off'), pairs)  1.92 us
    reshape x1, local copies, waits for them, and re-layouts, second_conv(): b_second.reshape(hid, 1)  1.34 us
    dot_general x1, matrix products, first_conv(): jnp.einsum('hcuv,ci->uvhi', w_first[:, :channels], rows, preferred_elemen...  1.18 us
  transfers between devices with their start and end apart: 4, of which 3 were waited for; matrix products, arithmetic and copies ran while one was open for 8% of the time, Pallas kernels for 0%

profile of v6, /device:TPU:446, one launch (start us, length us, event | category | flops | bytes accessed | tf_op | source)
XLA Modules:
  0.0 51.4 jit_solution(15215048641357868155)
XLA Ops:
  0.0 2.5 %collective-permute-start = (bf16[1,1,64,128]{3,2,1,0:T(8,128)(2,1)}, bf16[1,1,64,128]{3,2,1,0:T(8,128)(2,1)S(1)}, u32[]{:S(2)}, u32[]{:S(2)}) collective-permute-start(bf16[1,1,64,128]{3,2,1,0:T(8,128)(2,1)} %param.5), channel_id=1, source_target_pairs={{0,8},{1,9},{2,10},{3,11},{4,12},{5,13},{6,14},{7,15},{8,16},{9,17... | collective-permute-start | bytes 49160 | tf_op jit(solution)/shard_map/ppermute | solution.py:25
  2.5 3.3 %collective-permute-start.1 = (bf16[1,1,64,128]{3,2,1,0:T(8,128)(2,1)}, bf16[1,1,64,128]{3,2,1,0:T(8,128)(2,1)S(1)}, u32[]{:S(2)}, u32[]{:S(2)}) collective-permute-start(bf16[1,1,64,128]{3,2,1,0:T(8,128)(2,1)} %param.5), channel_id=1, source_target_pairs={{8,0},{9,1},{10,2},{11,3},{12,4},{13,5},{14,6},{15,7},{16,8},{17,9... | collective-permute-start | bytes 49160 | tf_op jit(solution)/shard_map/ppermute | solution.py:25
  5.9 3.3 %collective-permute-start.2 = (bf16[1,1,64,128]{3,2,1,0:T(8,128)(2,1)}, bf16[1,1,64,128]{3,2,1,0:T(8,128)(2,1)S(1)}, u32[]{:S(2)}, u32[]{:S(2)}) collective-permute-start(bf16[1,1,64,128]{3,2,1,0:T(8,128)(2,1)} %param.5), channel_id=1, source_target_pairs={{16,0},{17,1},{18,2},{19,3},{20,4},{21,5},{22,6},{23,7},{24,8},{25... | collective-permute-start | bytes 49160 | tf_op jit(solution)/shard_map/ppermute | solution.py:25
  9.3 0.2 convolution_convert_fusion
  9.5 0.1 convolution_convert_fusion.1
  9.9 0.1 fusion.13
  10.3 1.3 %copy.32.b_ref = f32[48,1]{1,0:T(8,128)} copy(f32[48,1]{0,1:T(1,128)} %bitcast.143) | data formatting | bytes 384 | tf_op jit(solution)/shard_map/reshape | solution.py:120
  11.7 0.9 %collective-permute-done.1 = bf16[1,1,64,128]{3,2,1,0:T(8,128)(2,1)S(1)} collective-permute-done((bf16[1,1,64,128]{3,2,1,0:T(8,128)(2,1)}, bf16[1,1,64,128]{3,2,1,0:T(8,128)(2,1)S(1)}, u32[]{:S(2)}, u32[]{:S(2)}) %collective-permute-start.1) | collective-permute-done | bytes 16416 | tf_op jit(solution)/shard_map/ppermute | solution.py:25
  12.6 1.2 %convolution_bitcast_fusion.1 = f32[3,3,48,140]{3,2,1,0:T(8,128)S(1)} fusion(bf16[48,128,3,3]{1,0,3,2:T(8,128)(2,1)} %param.6, bf16[1,64,128]{2,1,0:T(8,128)(2,1)S(1)} %bitcast.141, bf16[1,64,128]{2,1,0:T(8,128)(2,1)} %bitcast.139, bf16[1,64,128]{2,1,0:T(8,128)(2,1)S(1)} %bitcast.140), kind=kOutput, calls=%fused_computation.6 | convolution fusion | flops 7795200 | bytes 401664 | tf_op jit(solution)/shard_map/hcuv,ci->uvhi/dot_general | solution.py:57
  13.8 2.4 %collective-permute-done.2 = bf16[1,1,64,128]{3,2,1,0:T(8,128)(2,1)S(1)} collective-permute-done((bf16[1,1,64,128]{3,2,1,0:T(8,128)(2,1)}, bf16[1,1,64,128]{3,2,1,0:T(8,128)(2,1)S(1)}, u32[]{:S(2)}, u32[]{:S(2)}) %collective-permute-start.2) | collective-permute-done | bytes 16416 | tf_op jit(solution)/shard_map/ppermute | solution.py:25
  16.2 0.7 %pad_maximum_fusion.2 = bf16[4,1,64,128]{3,2,1,0:T(8,128)(2,1)S(1)} fusion(bf16[1,1,64,128]{3,2,1,0:T(8,128)(2,1)S(1)} %collective-permute-done.2, bf16[1,1,64,128]{3,2,1,0:T(8,128)(2,1)S(1)} %collective-permute-done.1, bf16[1,1,64,128]{3,2,1,0:T(8,128)(2,1)} %param.5, bf16[1,1,64,128]{3,2,1,0:T(8,128)(2,1)S(1)} %collective-permute-done), kind=kLoop, calls=%fused_computation.44 | loop fusion | flops 98304 | bytes 131072 | tf_op jit(solution)/shard_map/concatenate | solution.py:138
  16.9 1.9 %collective-permute-start.3 = (bf16[4,1,64,128]{3,2,1,0:T(8,128)(2,1)S(1)}, bf16[4,1,64,128]{3,2,1,0:T(8,128)(2,1)S(1)}, u32[]{:S(2)}, u32[]{:S(2)}) collective-permute-start(bf16[4,1,64,128]{3,2,1,0:T(8,128)(2,1)S(1)} %pad_maximum_fusion.2), channel_id=1, source_target_pairs={{10,2},{19,3},{28,4},{37,5},{46,6},{55,7},{18,10},{27,11},{36,12},... | collective-permute-start | bytes 196616 | tf_op jit(solution)/shard_map/ppermute | solution.py:145
  18.9 0.1 slice_bitcast_fusion.3
  19.0 0.1 reduce-precision_convert_fusion.1
  19.2 0.5 copy.28
  19.7 8.5 %collective-permute-done.3 = bf16[4,1,64,128]{3,2,1,0:T(8,128)(2,1)S(1)} collective-permute-done((bf16[4,1,64,128]{3,2,1,0:T(8,128)(2,1)S(1)}, bf16[4,1,64,128]{3,2,1,0:T(8,128)(2,1)S(1)}, u32[]{:S(2)}, u32[]{:S(2)}) %collective-permute-start.3) | collective-permute-done | bytes 65568 | tf_op jit(solution)/shard_map/ppermute | solution.py:145
  28.2 0.8 %fusion.16 = bf16[3,1,64,128]{3,2,1,0:T(8,128)(2,1)S(1)} fusion(bf16[4,1,64,128]{3,2,1,0:T(8,128)(2,1)S(1)} %collective-permute-done.3, bf16[1,1,64,128]{3,2,1,0:T(8,128)(2,1)S(1)} %collective-permute-done.1, bf16[1,1,64,128]{3,2,1,0:T(8,128)(2,1)} %param.5, bf16[1,1,64,128]{3,2,1,0:T(8,128)(2,1)S(1)} %collective-permute-done, ...), kind=kLoop, calls=%fused_computation.46 | loop fusion | flops 147456 | bytes 163842 | tf_op jit(solution)/shard_map/jit(_where)/select_n | solution.py:146
  29.0 1.2 %convolution_bitcast_fusion = f32[3,3,48,140]{3,2,1,0:T(8,128)S(1)} fusion(bf16[48,128,3,3]{1,0,3,2:T(8,128)(2,1)} %param.6, bf16[1,64,128]{2,1,0:T(8,128)(2,1)S(1)} %get-tuple-element.16, bf16[1,64,128]{2,1,0:T(8,128)(2,1)S(1)} %get-tuple-element.17, bf16[1,64,128]{2,1,0:T(8,128)(2,1)S(1)} %get-tuple-element.15), kind=kOutput, calls=%fused_computation.5 | convolution fusion | flops 7795200 | bytes 401664 | tf_op jit(solution)/shard_map/hcuv,cj->uvhj/dot_general | solution.py:58
  30.3 0.1 slice.162
  30.4 0.1 slice.165
  30.5 0.1 reduce-precision_convert_fusion
  30.7 1.1 %fusion.4 = f32[136,48,136]{2,0,1:T(8,128)S(1)} fusion(bf16[18,48,136]{2,1,0:T(8,128)(2,1)S(1)} %pad_maximum_fusion.1, bf16[136,9]{0,1:T(8,128)(2,1)S(1)} %convert_element_type.38), kind=kOutput, calls=%fused_computation.13 | convolution fusion | flops 31970880 | bytes 3788688 | tf_op jit(solution)/shard_map/ik,khj->ihj/dot_general | solution.py:83
  31.8 5.1 %fusion.3.hidden_ref = bf16[136,48,136]{2,1,0:T(8,128)(2,1)} fusion(f32[136,48,136]{2,0,1:T(8,128)S(1)} %fusion.4, f32[48]{0:T(128)S(1)} %copy-done, pred[136,136]{1,0:T(8,128)(4,1)S(1)} %fusion.13, bf16[136,48,18]{1,2,0:T(8,128)(2,1)S(1)} %copy.28, bf16[9,136]{1,0:T(8,128)(2,1)S(1)} %convert_element_type.36), kind=kOutput, calls=%fused_computation.4 | convolution fusion | flops 36409920 | bytes 5582992 | tf_op jit(solution)/shard_map/ihk,kj->ihj/dot_general | solution.py:81
  36.9 14.5 %shard_map.55 = bf16[48,128,128]{2,1,0:T(8,128)(2,1)} custom-call(bf16[9,48,48]{2,1,0:T(8,128)(2,1)} %bitcast.142, f32[48,1]{1,0:T(8,128)} %copy.32.b_ref, bf16[136,48,136]{2,1,0:T(8,128)(2,1)} %fusion.3.hidden_ref), custom_call_target="tpu_custom_call" | custom-call | tf_op jit(solution)/shard_map/pallas_call | solution.py:110
  (40 shorter events, 0.8 us)
Async XLA Ops:
  0.0 11.7 %collective-permute-start = (bf16[1,1,64,128]{3,2,1,0:T(8,128)(2,1)}, bf16[1,1,64,128]{3,2,1,0:T(8,128)(2,1)S(1)}, u32[]{:S(2)}, u32[]{:S(2)}) collective-permute-start(bf16[1,1,64,128]{3,2,1,0:T(8,128)(2,1)} %param.5), channel_id=1, source_target_pairs={{0,8},{1,9},{2,10},{3,11},{4,12},{5,13},{6,14},{7,15},{8,16},{9,17... | collective-permute-start | bytes 49160 | tf_op jit(solution)/shard_map/ppermute | solution.py:25
  2.5 10.1 %collective-permute-start.1 = (bf16[1,1,64,128]{3,2,1,0:T(8,128)(2,1)}, bf16[1,1,64,128]{3,2,1,0:T(8,128)(2,1)S(1)}, u32[]{:S(2)}, u32[]{:S(2)}) collective-permute-start(bf16[1,1,64,128]{3,2,1,0:T(8,128)(2,1)} %param.5), channel_id=1, source_target_pairs={{8,0},{9,1},{10,2},{11,3},{12,4},{13,5},{14,6},{15,7},{16,8},{17,9... | collective-permute-start | bytes 49160 | tf_op jit(solution)/shard_map/ppermute | solution.py:25
  5.9 10.4 %collective-permute-start.2 = (bf16[1,1,64,128]{3,2,1,0:T(8,128)(2,1)}, bf16[1,1,64,128]{3,2,1,0:T(8,128)(2,1)S(1)}, u32[]{:S(2)}, u32[]{:S(2)}) collective-permute-start(bf16[1,1,64,128]{3,2,1,0:T(8,128)(2,1)} %param.5), channel_id=1, source_target_pairs={{16,0},{17,1},{18,2},{19,3},{20,4},{21,5},{22,6},{23,7},{24,8},{25... | collective-permute-start | bytes 49160 | tf_op jit(solution)/shard_map/ppermute | solution.py:25
  16.9 11.3 %collective-permute-start.3 = (bf16[4,1,64,128]{3,2,1,0:T(8,128)(2,1)S(1)}, bf16[4,1,64,128]{3,2,1,0:T(8,128)(2,1)S(1)}, u32[]{:S(2)}, u32[]{:S(2)}) collective-permute-start(bf16[4,1,64,128]{3,2,1,0:T(8,128)(2,1)S(1)} %pad_maximum_fusion.2), channel_id=1, source_target_pairs={{10,2},{19,3},{28,4},{37,5},{46,6},{55,7},{18,10},{27,11},{36,12},... | collective-permute-start | bytes 196616 | tf_op jit(solution)/shard_map/ppermute | solution.py:145
  19.2 12.6 %copy-start = (f32[48]{0:T(128)S(1)}, f32[48]{0:T(128)}, u32[]{:S(2)}) copy-start(f32[48]{0:T(128)} %param.7) | copy-start | bytes 580

commit v7 on v5

--- a/solution.py
+++ b/solution.py
@@ -85,7 +85,7 @@
     return term_row + term_col
 
 
-ROWS_PER_STEP = 8
+ROWS_PER_STEP = 16
 
 
 def second_conv_kernel(w_ref, b_ref, hidden_ref, out_ref):

time: 51.4 us -> 50.5 us (0.982)
  Pallas kernels: 14.5 us -> 13.6 us
    pallas_call x1, Pallas kernels: 14.5 us -> 13.6 us  [second_conv(): pl.pallas_call(second_conv_kernel, grid=(width // ROWS_PER_STEP,), in_spe...]
where the time goes in v7:
time: 50.5 us; the launch traced here: 50.1 us
  starting transfers between devices  23.3 us (46%)
  Pallas kernels  13.6 us (27%)
  matrix products  8.85 us (18%)
  local copies, waits for them, and re-layouts  2.64 us (5%)
  other arithmetic  1.38 us (3%)
    ppermute x5, starting transfers between devices, fetch(): moved = lax.ppermute(trunk, ('diag', 'off'), pairs)  23.3 us
    pallas_call x1, Pallas kernels, second_conv(): pl.pallas_call(second_conv_kernel, grid=(width // ROWS_PER_STEP,), in_spe...  13.6 us
    dot_general x1, matrix products, first_conv(): jnp.einsum('ihk,kj->ihj', p_row_both, jnp.concatenate([q_col, q_col], axi...  5.12 us
    reshape x1, local copies, waits for them, and re-layouts, second_conv(): b_second.reshape(hid, 1)  1.34 us
    dot_general x1, matrix products, first_conv(): jnp.einsum('hcuv,ci->uvhi', w_first[:, :channels], rows, preferred_elemen...  1.19 us
    dot_general x1, matrix products, first_conv(): jnp.einsum('hcuv,cj->uvhj', w_first[:, channels:], cols, preferred_elemen...  1.17 us
    dot_general x1, matrix products, first_conv(): jnp.einsum('ik,khj->ihj', jnp.concatenate([q_row, q_row], axis=1), p_col_...  1.06 us
  transfers between devices with their start and end apart: 5, of which 0 were waited for; matrix products, arithmetic and copies ran while one was open for 10% of the time, Pallas kernels for 0%

profile of v7, /device:TPU:452, one launch (start us, length us, event | category | flops | bytes accessed | tf_op | source)
XLA Modules:
  0.0 50.1 jit_solution(8763912422472840509)
XLA Ops:
  0.0 3.1 %collective-permute-start = (bf16[1,1,64,128]{3,2,1,0:T(8,128)(2,1)}, bf16[1,1,64,128]{3,2,1,0:T(8,128)(2,1)S(1)}, u32[]{:S(2)}, u32[]{:S(2)}) collective-permute-start(bf16[1,1,64,128]{3,2,1,0:T(8,128)(2,1)} %param.5), channel_id=1, source_target_pairs={{0,8},{1,9},{2,10},{3,11},{4,12},{5,13},{6,14},{7,15},{8,16},{9,17... | collective-permute-start | bytes 49160 | tf_op jit(solution)/shard_map/ppermute | solution.py:25
  3.1 2.7 %collective-permute-start.1 = (bf16[1,1,64,128]{3,2,1,0:T(8,128)(2,1)}, bf16[1,1,64,128]{3,2,1,0:T(8,128)(2,1)S(1)}, u32[]{:S(2)}, u32[]{:S(2)}) collective-permute-start(bf16[1,1,64,128]{3,2,1,0:T(8,128)(2,1)} %param.5), channel_id=1, source_target_pairs={{8,0},{9,1},{10,2},{11,3},{12,4},{13,5},{14,6},{15,7},{16,8},{17,9... | collective-permute-start | bytes 49160 | tf_op jit(solution)/shard_map/ppermute | solution.py:25
  5.9 5.3 %collective-permute-start.2 = (bf16[1,1,64,128]{3,2,1,0:T(8,128)(2,1)}, bf16[1,1,64,128]{3,2,1,0:T(8,128)(2,1)S(1)}, u32[]{:S(2)}, u32[]{:S(2)}) collective-permute-start(bf16[1,1,64,128]{3,2,1,0:T(8,128)(2,1)} %param.5), channel_id=1, source_target_pairs={{10,2},{19,3},{28,4},{37,5},{46,6},{55,7},{0,8},{18,10},{27,11},{3... | collective-permute-start | bytes 49160 | tf_op jit(solution)/shard_map/ppermute | solution.py:25
  11.2 6.2 %collective-permute-start.3 = (bf16[1,1,64,128]{3,2,1,0:T(8,128)(2,1)}, bf16[1,1,64,128]{3,2,1,0:T(8,128)(2,1)S(1)}, u32[]{:S(2)}, u32[]{:S(2)}) collective-permute-start(bf16[1,1,64,128]{3,2,1,0:T(8,128)(2,1)} %param.5), channel_id=1, source_target_pairs={{9,1},{18,2},{27,3},{36,4},{45,5},{54,6},{63,7},{17,9},{26,10},{35... | collective-permute-start | bytes 49160 | tf_op jit(solution)/shard_map/ppermute | solution.py:25
  17.4 5.9 %collective-permute-start.4 = (bf16[1,1,64,128]{3,2,1,0:T(8,128)(2,1)}, bf16[1,1,64,128]{3,2,1,0:T(8,128)(2,1)S(1)}, u32[]{:S(2)}, u32[]{:S(2)}) collective-permute-start(bf16[1,1,64,128]{3,2,1,0:T(8,128)(2,1)} %param.5), channel_id=1, source_target_pairs={{8,0},{17,1},{26,2},{35,3},{44,4},{53,5},{62,6},{71,7},{16,8},{25,... | collective-permute-start | bytes 49160 | tf_op jit(solution)/shard_map/ppermute | solution.py:25
  23.4 0.2 convolution_convert_fusion
  23.6 0.1 convolution_convert_fusion.1
  23.9 0.1 slice_bitcast_fusion.14
  24.1 0.1 fusion.13
  24.5 1.3 %copy.32.b_ref = f32[48,1]{1,0:T(8,128)} copy(f32[48,1]{0,1:T(1,128)} %bitcast.143) | data formatting | bytes 384 | tf_op jit(solution)/shard_map/reshape | solution.py:120
  25.8 1.2 %convolution_bitcast_fusion.1 = f32[3,3,48,140]{3,2,1,0:T(8,128)S(1)} fusion(bf16[48,128,3,3]{1,0,3,2:T(8,128)(2,1)} %param.6, bf16[1,64,128]{2,1,0:T(8,128)(2,1)S(1)} %bitcast.142, bf16[1,64,128]{2,1,0:T(8,128)(2,1)} %bitcast.139, bf16[1,64,128]{2,1,0:T(8,128)(2,1)S(1)} %bitcast.141), kind=kOutput, calls=%fused_computation.6 | convolution fusion | flops 7795200 | bytes 401664 | tf_op jit(solution)/shard_map/hcuv,ci->uvhi/dot_general | solution.py:57
  27.0 0.1 slice_bitcast_fusion.3
  27.2 0.1 reduce-precision_convert_fusion.1
  27.4 0.7 %select_bitcast_fusion.1 = (bf16[1,64,128]{2,1,0:T(8,128)(2,1)S(1)}, bf16[1,64,128]{2,1,0:T(8,128)(2,1)S(1)}) fusion(bf16[1,1,64,128]{3,2,1,0:T(8,128)(2,1)} %param.5, bf16[1,1,64,128]{3,2,1,0:T(8,128)(2,1)S(1)} %collective-permute-done.2, pred[]{:T(512)S(6)} %eq.38, bf16[1,1,64,128]{3,2,1,0:T(8,128)(2,1)S(1)} %collective-permute-done.3, pred[]{:T(512)S(6)} %eq.39), kind=kLoop, calls=%fused_computation.53 | loop fusion | flops 16384 | bytes 81922 | tf_op jit(solution)/shard_map/squeeze | solution.py:142
  28.1 0.1 pad_maximum_fusion
  28.2 0.5 copy.28
  28.7 1.2 %convolution_bitcast_fusion = f32[3,3,48,140]{3,2,1,0:T(8,128)S(1)} fusion(bf16[48,128,3,3]{1,0,3,2:T(8,128)(2,1)} %param.6, bf16[1,64,128]{2,1,0:T(8,128)(2,1)S(1)} %bitcast.140, bf16[1,64,128]{2,1,0:T(8,128)(2,1)S(1)} %get-tuple-element.16, bf16[1,64,128]{2,1,0:T(8,128)(2,1)S(1)} %get-tuple-element.15), kind=kOutput, calls=%fused_computation.5 | convolution fusion | flops 7795200 | bytes 401664 | tf_op jit(solution)/shard_map/hcuv,cj->uvhj/dot_general | solution.py:58
  29.9 0.1 slice.138
  30.0 0.1 slice.141
  30.1 0.1 reduce-precision_convert_fusion
  30.2 0.1 pad_maximum_fusion.1
  30.3 1.1 %fusion.4 = f32[136,48,136]{2,0,1:T(8,128)S(1)} fusion(bf16[18,48,136]{2,1,0:T(8,128)(2,1)S(1)} %pad_maximum_fusion.1, bf16[136,9]{0,1:T(8,128)(2,1)S(1)} %convert_element_type.38), kind=kOutput, calls=%fused_computation.13 | convolution fusion | flops 31970880 | bytes 3788688 | tf_op jit(solution)/shard_map/ik,khj->ihj/dot_general | solution.py:83
  31.4 5.1 %fusion.3.hidden_ref = bf16[136,48,136]{2,1,0:T(8,128)(2,1)} fusion(f32[136,48,136]{2,0,1:T(8,128)S(1)} %fusion.4, f32[48]{0:T(128)S(1)} %copy-done, pred[136,136]{1,0:T(8,128)(4,1)S(1)} %fusion.13, bf16[136,48,18]{1,2,0:T(8,128)(2,1)S(1)} %copy.28, bf16[9,136]{1,0:T(8,128)(2,1)S(1)} %convert_element_type.36), kind=kOutput, calls=%fused_computation.4 | convolution fusion | flops 36409920 | bytes 5582992 | tf_op jit(solution)/shard_map/ihk,kj->ihj/dot_general | solution.py:81
  36.5 13.6 %shard_map.55 = bf16[48,128,128]{2,1,0:T(8,128)(2,1)} custom-call(bf16[9,48,48]{2,1,0:T(8,128)(2,1)} %bitcast.138, f32[48,1]{1,0:T(8,128)} %copy.32.b_ref, bf16[136,48,136]{2,1,0:T(8,128)(2,1)} %fusion.3.hidden_ref), custom_call_target="tpu_custom_call" | custom-call | tf_op jit(solution)/shard_map/pallas_call | solution.py:110
  (40 shorter events, 0.6 us)
Async XLA Ops:
  0.0 25.8 %collective-permute-start = (bf16[1,1,64,128]{3,2,1,0:T(8,128)(2,1)}, bf16[1,1,64,128]{3,2,1,0:T(8,128)(2,1)S(1)}, u32[]{:S(2)}, u32[]{:S(2)}) collective-permute-start(bf16[1,1,64,128]{3,2,1,0:T(8,128)(2,1)} %param.5), channel_id=1, source_target_pairs={{0,8},{1,9},{2,10},{3,11},{4,12},{5,13},{6,14},{7,15},{8,16},{9,17... | collective-permute-start | bytes 49160 | tf_op jit(solution)/shard_map/ppermute | solution.py:25
  3.1 22.7 %collective-permute-start.1 = (bf16[1,1,64,128]{3,2,1,0:T(8,128)(2,1)}, bf16[1,1,64,128]{3,2,1,0:T(8,128)(2,1)S(1)}, u32[]{:S(2)}, u32[]{:S(2)}) collective-permute-start(bf16[1,1,64,128]{3,2,1,0:T(8,128)(2,1)} %param.5), channel_id=1, source_target_pairs={{8,0},{9,1},{10,2},{11,3},{12,4},{13,5},{14,6},{15,7},{16,8},{17,9... | collective-permute-start | bytes 49160 | tf_op jit(solution)/shard_map/ppermute | solution.py:25
  5.9 21.5 %collective-permute-start.2 = (bf16[1,1,64,128]{3,2,1,0:T(8,128)(2,1)}, bf16[1,1,64,128]{3,2,1,0:T(8,128)(2,1)S(1)}, u32[]{:S(2)}, u32[]{:S(2)}) collective-permute-start(bf16[1,1,64,128]{3,2,1,0:T(8,128)(2,1)} %param.5), channel_id=1, source_target_pairs={{10,2},{19,3},{28,4},{37,5},{46,6},{55,7},{0,8},{18,10},{27,11},{3... | collective-permute-start | bytes 49160 | tf_op jit(solution)/shard_map/ppermute | solution.py:25
  11.2 16.2 %collective-permute-start.3 = (bf16[1,1,64,128]{3,2,1,0:T(8,128)(2,1)}, bf16[1,1,64,128]{3,2,1,0:T(8,128)(2,1)S(1)}, u32[]{:S(2)}, u32[]{:S(2)}) collective-permute-start(bf16[1,1,64,128]{3,2,1,0:T(8,128)(2,1)} %param.5), channel_id=1, source_target_pairs={{9,1},{18,2},{27,3},{36,4},{45,5},{54,6},{63,7},{17,9},{26,10},{35... | collective-permute-start | bytes 49160 | tf_op jit(solution)/shard_map/ppermute | solution.py:25
  17.4 11.2 %collective-permute-start.4 = (bf16[1,1,64,128]{3,2,1,0:T(8,128)(2,1)}, bf16[1,1,64,128]{3,2,1,0:T(8,128)(2,1)S(1)}, u32[]{:S(2)}, u32[]{:S(2)}) collective-permute-start(bf16[1,1,64,128]{3,2,1,0:T(8,128)(2,1)} %param.5), channel_id=1, source_target_pairs={{8,0},{17,1},{26,2},{35,3},{44,4},{53,5},{62,6},{71,7},{16,8},{25,... | collective-permute-start | bytes 49160 | tf_op jit(solution)/shard_map/ppermute | solution.py:25
  28.1 3.3 %copy-start = (f32[48]{0:T(128)S(1)}, f32[48]{0:T(128)}, u32[]{:S(2)}) copy-start(f32[48]{0:T(128)} %param.7) | copy-start | bytes 580

commit v8 on v7

--- a/solution.py
+++ b/solution.py
@@ -85,7 +85,7 @@
     return term_row + term_col
 
 
-ROWS_PER_STEP = 16
+ROWS_PER_STEP = 32
 
 
 def second_conv_kernel(w_ref, b_ref, hidden_ref, out_ref):

time: 50.5 us -> 49.1 us (0.972)
  Pallas kernels: 13.6 us -> 12.2 us
    pallas_call x1, Pallas kernels: 13.6 us -> 12.2 us  [second_conv(): pl.pallas_call(second_conv_kernel, grid=(width // ROWS_PER_STEP,), in_spe...]
where the time goes in v8:
time: 49.1 us; the launch traced here: 48.7 us
  starting transfers between devices  23.3 us (47%)
  Pallas kernels  12.2 us (25%)
  matrix products  8.85 us (18%)
  local copies, waits for them, and re-layouts  2.64 us (5%)
  other arithmetic  1.38 us (3%)
    ppermute x5, starting transfers between devices, fetch(): moved = lax.ppermute(trunk, ('diag', 'off'), pairs)  23.3 us
    pallas_call x1, Pallas kernels, second_conv(): pl.pallas_call(second_conv_kernel, grid=(width // ROWS_PER_STEP,), in_spe...  12.2 us
    dot_general x1, matrix products, first_conv(): jnp.einsum('ihk,kj->ihj', p_row_both, jnp.concatenate([q_col, q_col], axi...  5.12 us
    reshape x1, local copies, waits for them, and re-layouts, second_conv(): b_second.reshape(hid, 1)  1.34 us
    dot_general x1, matrix products, first_conv(): jnp.einsum('hcuv,ci->uvhi', w_first[:, :channels], rows, preferred_elemen...  1.19 us
    dot_general x1, matrix products, first_conv(): jnp.einsum('hcuv,cj->uvhj', w_first[:, channels:], cols, preferred_elemen...  1.17 us
    dot_general x1, matrix products, first_conv(): jnp.einsum('ik,khj->ihj', jnp.concatenate([q_row, q_row], axis=1), p_col_...  1.06 us
  transfers between devices with their start and end apart: 5, of which 0 were waited for; matrix products, arithmetic and copies ran while one was open for 10% of the time, Pallas kernels for 0%

profile of v8, /device:TPU:452, one launch (start us, length us, event | category | flops | bytes accessed | tf_op | source)
XLA Modules:
  0.0 48.7 jit_solution(13244553035908513280)
XLA Ops:
  0.0 3.1 %collective-permute-start = (bf16[1,1,64,128]{3,2,1,0:T(8,128)(2,1)}, bf16[1,1,64,128]{3,2,1,0:T(8,128)(2,1)S(1)}, u32[]{:S(2)}, u32[]{:S(2)}) collective-permute-start(bf16[1,1,64,128]{3,2,1,0:T(8,128)(2,1)} %param.5), channel_id=1, source_target_pairs={{0,8},{1,9},{2,10},{3,11},{4,12},{5,13},{6,14},{7,15},{8,16},{9,17... | collective-permute-start | bytes 49160 | tf_op jit(solution)/shard_map/ppermute | solution.py:25
  3.1 2.7 %collective-permute-start.1 = (bf16[1,1,64,128]{3,2,1,0:T(8,128)(2,1)}, bf16[1,1,64,128]{3,2,1,0:T(8,128)(2,1)S(1)}, u32[]{:S(2)}, u32[]{:S(2)}) collective-permute-start(bf16[1,1,64,128]{3,2,1,0:T(8,128)(2,1)} %param.5), channel_id=1, source_target_pairs={{8,0},{9,1},{10,2},{11,3},{12,4},{13,5},{14,6},{15,7},{16,8},{17,9... | collective-permute-start | bytes 49160 | tf_op jit(solution)/shard_map/ppermute | solution.py:25
  5.9 5.3 %collective-permute-start.2 = (bf16[1,1,64,128]{3,2,1,0:T(8,128)(2,1)}, bf16[1,1,64,128]{3,2,1,0:T(8,128)(2,1)S(1)}, u32[]{:S(2)}, u32[]{:S(2)}) collective-permute-start(bf16[1,1,64,128]{3,2,1,0:T(8,128)(2,1)} %param.5), channel_id=1, source_target_pairs={{10,2},{19,3},{28,4},{37,5},{46,6},{55,7},{0,8},{18,10},{27,11},{3... | collective-permute-start | bytes 49160 | tf_op jit(solution)/shard_map/ppermute | solution.py:25
  11.2 6.2 %collective-permute-start.3 = (bf16[1,1,64,128]{3,2,1,0:T(8,128)(2,1)}, bf16[1,1,64,128]{3,2,1,0:T(8,128)(2,1)S(1)}, u32[]{:S(2)}, u32[]{:S(2)}) collective-permute-start(bf16[1,1,64,128]{3,2,1,0:T(8,128)(2,1)} %param.5), channel_id=1, source_target_pairs={{9,1},{18,2},{27,3},{36,4},{45,5},{54,6},{63,7},{17,9},{26,10},{35... | collective-permute-start | bytes 49160 | tf_op jit(solution)/shard_map/ppermute | solution.py:25
  17.4 5.9 %collective-permute-start.4 = (bf16[1,1,64,128]{3,2,1,0:T(8,128)(2,1)}, bf16[1,1,64,128]{3,2,1,0:T(8,128)(2,1)S(1)}, u32[]{:S(2)}, u32[]{:S(2)}) collective-permute-start(bf16[1,1,64,128]{3,2,1,0:T(8,128)(2,1)} %param.5), channel_id=1, source_target_pairs={{8,0},{17,1},{26,2},{35,3},{44,4},{53,5},{62,6},{71,7},{16,8},{25,... | collective-permute-start | bytes 49160 | tf_op jit(solution)/shard_map/ppermute | solution.py:25
  23.4 0.2 convolution_convert_fusion
  23.6 0.1 convolution_convert_fusion.1
  23.9 0.1 slice_bitcast_fusion.14
  24.1 0.1 fusion.13
  24.5 1.3 %copy.32.b_ref = f32[48,1]{1,0:T(8,128)} copy(f32[48,1]{0,1:T(1,128)} %bitcast.143) | data formatting | bytes 384 | tf_op jit(solution)/shard_map/reshape | solution.py:120
  25.8 1.2 %convolution_bitcast_fusion.1 = f32[3,3,48,140]{3,2,1,0:T(8,128)S(1)} fusion(bf16[48,128,3,3]{1,0,3,2:T(8,128)(2,1)} %param.6, bf16[1,64,128]{2,1,0:T(8,128)(2,1)S(1)} %bitcast.142, bf16[1,64,128]{2,1,0:T(8,128)(2,1)} %bitcast.139, bf16[1,64,128]{2,1,0:T(8,128)(2,1)S(1)} %bitcast.141), kind=kOutput, calls=%fused_computation.6 | convolution fusion | flops 7795200 | bytes 401664 | tf_op jit(solution)/shard_map/hcuv,ci->uvhi/dot_general | solution.py:57
  27.0 0.1 slice_bitcast_fusion.3
  27.2 0.1 reduce-precision_convert_fusion.1
  27.4 0.7 %select_bitcast_fusion.1 = (bf16[1,64,128]{2,1,0:T(8,128)(2,1)S(1)}, bf16[1,64,128]{2,1,0:T(8,128)(2,1)S(1)}) fusion(bf16[1,1,64,128]{3,2,1,0:T(8,128)(2,1)} %param.5, bf16[1,1,64,128]{3,2,1,0:T(8,128)(2,1)S(1)} %collective-permute-done.2, pred[]{:T(512)S(6)} %eq.38, bf16[1,1,64,128]{3,2,1,0:T(8,128)(2,1)S(1)} %collective-permute-done.3, pred[]{:T(512)S(6)} %eq.39), kind=kLoop, calls=%fused_computation.53 | loop fusion | flops 16384 | bytes 81922 | tf_op jit(solution)/shard_map/squeeze | solution.py:142
  28.1 0.1 pad_maximum_fusion
  28.2 0.5 copy.28
  28.7 1.2 %convolution_bitcast_fusion = f32[3,3,48,140]{3,2,1,0:T(8,128)S(1)} fusion(bf16[48,128,3,3]{1,0,3,2:T(8,128)(2,1)} %param.6, bf16[1,64,128]{2,1,0:T(8,128)(2,1)S(1)} %bitcast.140, bf16[1,64,128]{2,1,0:T(8,128)(2,1)S(1)} %get-tuple-element.16, bf16[1,64,128]{2,1,0:T(8,128)(2,1)S(1)} %get-tuple-element.15), kind=kOutput, calls=%fused_computation.5 | convolution fusion | flops 7795200 | bytes 401664 | tf_op jit(solution)/shard_map/hcuv,cj->uvhj/dot_general | solution.py:58
  29.9 0.1 slice.138
  30.0 0.1 slice.141
  30.1 0.1 reduce-precision_convert_fusion
  30.2 0.1 pad_maximum_fusion.1
  30.3 1.1 %fusion.4 = f32[136,48,136]{2,0,1:T(8,128)S(1)} fusion(bf16[18,48,136]{2,1,0:T(8,128)(2,1)S(1)} %pad_maximum_fusion.1, bf16[136,9]{0,1:T(8,128)(2,1)S(1)} %convert_element_type.38), kind=kOutput, calls=%fused_computation.13 | convolution fusion | flops 31970880 | bytes 3788688 | tf_op jit(solution)/shard_map/ik,khj->ihj/dot_general | solution.py:83
  31.4 5.1 %fusion.3.hidden_ref = bf16[136,48,136]{2,1,0:T(8,128)(2,1)} fusion(f32[136,48,136]{2,0,1:T(8,128)S(1)} %fusion.4, f32[48]{0:T(128)S(1)} %copy-done, pred[136,136]{1,0:T(8,128)(4,1)S(1)} %fusion.13, bf16[136,48,18]{1,2,0:T(8,128)(2,1)S(1)} %copy.28, bf16[9,136]{1,0:T(8,128)(2,1)S(1)} %convert_element_type.36), kind=kOutput, calls=%fused_computation.4 | convolution fusion | flops 36409920 | bytes 5582992 | tf_op jit(solution)/shard_map/ihk,kj->ihj/dot_general | solution.py:81
  36.5 12.2 %shard_map.55 = bf16[48,128,128]{2,1,0:T(8,128)(2,1)} custom-call(bf16[9,48,48]{2,1,0:T(8,128)(2,1)} %bitcast.138, f32[48,1]{1,0:T(8,128)} %copy.32.b_ref, bf16[136,48,136]{2,1,0:T(8,128)(2,1)} %fusion.3.hidden_ref), custom_call_target="tpu_custom_call" | custom-call | tf_op jit(solution)/shard_map/pallas_call | solution.py:110
  (40 shorter events, 0.6 us)
Async XLA Ops:
  0.0 25.8 %collective-permute-start = (bf16[1,1,64,128]{3,2,1,0:T(8,128)(2,1)}, bf16[1,1,64,128]{3,2,1,0:T(8,128)(2,1)S(1)}, u32[]{:S(2)}, u32[]{:S(2)}) collective-permute-start(bf16[1,1,64,128]{3,2,1,0:T(8,128)(2,1)} %param.5), channel_id=1, source_target_pairs={{0,8},{1,9},{2,10},{3,11},{4,12},{5,13},{6,14},{7,15},{8,16},{9,17... | collective-permute-start | bytes 49160 | tf_op jit(solution)/shard_map/ppermute | solution.py:25
  3.1 22.7 %collective-permute-start.1 = (bf16[1,1,64,128]{3,2,1,0:T(8,128)(2,1)}, bf16[1,1,64,128]{3,2,1,0:T(8,128)(2,1)S(1)}, u32[]{:S(2)}, u32[]{:S(2)}) collective-permute-start(bf16[1,1,64,128]{3,2,1,0:T(8,128)(2,1)} %param.5), channel_id=1, source_target_pairs={{8,0},{9,1},{10,2},{11,3},{12,4},{13,5},{14,6},{15,7},{16,8},{17,9... | collective-permute-start | bytes 49160 | tf_op jit(solution)/shard_map/ppermute | solution.py:25
  5.9 21.5 %collective-permute-start.2 = (bf16[1,1,64,128]{3,2,1,0:T(8,128)(2,1)}, bf16[1,1,64,128]{3,2,1,0:T(8,128)(2,1)S(1)}, u32[]{:S(2)}, u32[]{:S(2)}) collective-permute-start(bf16[1,1,64,128]{3,2,1,0:T(8,128)(2,1)} %param.5), channel_id=1, source_target_pairs={{10,2},{19,3},{28,4},{37,5},{46,6},{55,7},{0,8},{18,10},{27,11},{3... | collective-permute-start | bytes 49160 | tf_op jit(solution)/shard_map/ppermute | solution.py:25
  11.2 16.2 %collective-permute-start.3 = (bf16[1,1,64,128]{3,2,1,0:T(8,128)(2,1)}, bf16[1,1,64,128]{3,2,1,0:T(8,128)(2,1)S(1)}, u32[]{:S(2)}, u32[]{:S(2)}) collective-permute-start(bf16[1,1,64,128]{3,2,1,0:T(8,128)(2,1)} %param.5), channel_id=1, source_target_pairs={{9,1},{18,2},{27,3},{36,4},{45,5},{54,6},{63,7},{17,9},{26,10},{35... | collective-permute-start | bytes 49160 | tf_op jit(solution)/shard_map/ppermute | solution.py:25
  17.4 11.2 %collective-permute-start.4 = (bf16[1,1,64,128]{3,2,1,0:T(8,128)(2,1)}, bf16[1,1,64,128]{3,2,1,0:T(8,128)(2,1)S(1)}, u32[]{:S(2)}, u32[]{:S(2)}) collective-permute-start(bf16[1,1,64,128]{3,2,1,0:T(8,128)(2,1)} %param.5), channel_id=1, source_target_pairs={{8,0},{17,1},{26,2},{35,3},{44,4},{53,5},{62,6},{71,7},{16,8},{25,... | collective-permute-start | bytes 49160 | tf_op jit(solution)/shard_map/ppermute | solution.py:25
  28.1 3.3 %copy-start = (f32[48]{0:T(128)S(1)}, f32[48]{0:T(128)}, u32[]{:S(2)}) copy-start(f32[48]{0:T(128)} %param.7) | copy-start | bytes 580
